TPU v7x, 256 devices: a whole 4x4x8 slice. The times are simulated.
256 devices in a mesh: row: 8 (over z_lo, x), rep: 32 (over z_hi, y, core).
Axes of the slice: x: 4, y: 4, z: 8 (z_hi: 4, z_lo: 2; z = z_hi * 2 + z_lo), core: 2. Of those that a mesh axis runs over, the one named last changes fastest.
Arguments:
- features: bfloat16 [32768, 128], P(('row', 'rep')), may hold values from -6 to 6
- block_values: bfloat16 [32768, 128, 128], P(('row', 'rep')), may hold values from -0.078125 to 0.078125
- block_rows: int32 [256, 128], P(('row', 'rep')), may hold values from 0 to 31, as said below
- block_cols: int32 [256, 128], P(('row', 'rep')), may hold values from 0 to 7, as said below
- block_count: int32 [256], replicated, may hold values from 16 to 128, as said below
- weight: bfloat16 [128, 256], replicated, may hold values from -0.5 to 0.5
- bias: float32 [256], replicated, may hold values from -3 to 3
Outputs:
- output: bfloat16 [32768, 256], P(('row', 'rep'))
Inputs may be any that keep to these rules, and one draw needn't show every extreme that they name: `block_rows`: no two slots of one device name the same row block and column section. `block_cols`: with block_rows, no two slots of one device name the same pair. `block_count`: the live slots of a device are its first ones; some device has all 128 slots live.
All inputs are finite; a program needn't handle non-finite values.
Results may differ from a plain program's by a relative error of at most 0.0046.
Values may be sent and summed in bfloat16 or wider, within the bound.
No kernel may reach another device: no remote copies, remote signals or barrier semaphores. Data moves between devices by JAX's collectives and lax.ppermute only.
A program may use at most 64 MiB of HBM per device.

v0:
```python
import jax
import jax.numpy as jnp
from jax import lax
from jax.experimental import pallas as pl
from jax.experimental.pallas import tpu as pltpu
from jax.sharding import PartitionSpec as P


GROUP = 64


def slot_kernel(rows_ref, cols_ref, count_ref, feats_ref, vals_ref, keep_ref, send_ref, acc_ref):
    g = pl.program_id(0)
    live = count_ref[0]
    row_index = lax.axis_index("row")
    core = lax.axis_index("rep") % 2
    x_size = feats_ref.shape[0] // 2
    lo = row_index // x_size
    xi = row_index % x_size
    row_top = acc_ref.shape[0] - 1

    @pl.when(g == 0)
    def _():
        acc_ref[...] = jnp.zeros_like(acc_ref)

    @pl.when(g * GROUP < live)
    def _():
        for s in range(GROUP):
            k = g * GROUP + s
            r = jnp.clip(rows_ref[k], 0, row_top)
            c = jnp.clip(cols_ref[k], 0, 2 * x_size - 1)
            spot = ((xi - c % x_size) % x_size) * 2 + ((c // x_size) ^ lo)
            prod = jnp.dot(vals_ref[s], feats_ref[spot], preferred_element_type=jnp.float32)
            acc_ref[r] += jnp.where(k < live, prod, 0.0)

    @pl.when(g == pl.num_programs(0) - 1)
    def _():
        for t in range(keep_ref.shape[0]):
            keep_ref[t] = acc_ref[2 * t + core]
            send_ref[t] = acc_ref[2 * t + 1 - core]


def accumulate_slots(rows, cols, count, feats, vals, rep_size):
    slot_total, blk, _ = vals.shape
    sections, _, width = feats.shape
    groups = slot_total // GROUP

    def vals_map(g, rows_ref, cols_ref, count_ref):
        last = jnp.maximum(count_ref[0] - 1, 0) // GROUP
        return (jnp.minimum(g, last), 0, 0)

    half = jax.ShapeDtypeStruct((rep_size // 2, blk, width), jnp.float32)
    half_spec = pl.BlockSpec((rep_size // 2, blk, width), lambda g, *_: (0, 0, 0))
    grid_spec = pltpu.PrefetchScalarGridSpec(
        num_scalar_prefetch=3,
        grid=(groups,),
        in_specs=[
            pl.BlockSpec((sections, blk, width), lambda g, *_: (0, 0, 0)),
            pl.BlockSpec((GROUP, blk, blk), vals_map),
        ],
        out_specs=[half_spec, half_spec],
        scratch_shapes=[pltpu.VMEM((rep_size, blk, width), jnp.float32)],
    )
    return pl.pallas_call(
        slot_kernel,
        grid_spec=grid_spec,
        out_shape=[half, half],
        compiler_params=pltpu.CompilerParams(dimension_semantics=("arbitrary",)),
        cost_estimate=pl.CostEstimate(
            flops=2 * slot_total * blk * blk * width,
            bytes_accessed=vals.size * 2 + feats.size * 2 + rep_size * blk * width * 4,
            transcendentals=0,
        ),
    )(rows, cols, count, feats, vals)


def gather_over_row(x):
    row_size = lax.axis_size("row")
    x_size = row_size // 2
    other = lax.ppermute(x, "row", [(s, (s + x_size) % row_size) for s in range(row_size)])
    pair = jnp.stack([x, other])
    parts = [pair]
    for d in range(1, x_size):
        perm = [(s, (s // x_size) * x_size + (s % x_size + d) % x_size) for s in range(row_size)]
        parts.append(lax.ppermute(pair, "row", perm))
    return jnp.concatenate(parts, axis=0)


def y_pairs(rep_size, d):
    return [(i, (i // 8) * 8 + (((i // 2) % 4 + d) % 4) * 2 + i % 2) for i in range(rep_size)]


def z_pairs(rep_size, z_size, d):
    return [(i, (((i // 8) + d) % z_size) * 8 + i % 8) for i in range(rep_size)]


def reduce_over_rep(keep, send):
    rep_size = 2 * keep.shape[0]
    z_size = rep_size // 8
    j = lax.axis_index("rep")
    y = (j // 2) % 4
    z = j // 8
    shape = (z_size, 4) + keep.shape[1:]
    x = keep.reshape(shape) + lax.ppermute(
        send.reshape(shape), "rep", [(i, i ^ 1) for i in range(rep_size)]
    )
    early = [d for d in range(1, z_size) if d < z_size - 1]
    late = [0] + [d for d in range(1, z_size) if d not in early]
    blocks = {}
    for shifts in (early, late):
        part = jnp.stack(
            [lax.dynamic_index_in_dim(x, (z + d) % z_size, 0, keepdims=False) for d in shifts]
        )
        acc = lax.dynamic_index_in_dim(part, y, 1, keepdims=False)
        got = [
            lax.ppermute(
                lax.dynamic_index_in_dim(part, (y + dy) % 4, 1, keepdims=False),
                "rep",
                y_pairs(rep_size, dy),
            )
            for dy in (1, 2, 3)
        ]
        for piece in got:
            acc = acc + piece
        for n, d in enumerate(shifts):
            blocks[d] = acc[n]
    out = blocks[0]
    for d in range(1, z_size):
        out = out + lax.ppermute(blocks[d], "rep", z_pairs(rep_size, z_size, d))
    return out


def layer(features, block_values, block_rows, block_cols, block_count, weight, bias):
    rep_size = lax.axis_size("rep")
    section_features = gather_over_row(features)
    device_index = lax.axis_index(("row", "rep"))
    live_count = lax.dynamic_slice_in_dim(block_count, device_index, 1, 0)
    keep, send = accumulate_slots(
        block_rows[0], block_cols[0], live_count, section_features, block_values, rep_size
    )
    summed = reduce_over_rep(keep, send)
    reduced = summed.astype(jnp.bfloat16)
    projected = jnp.dot(reduced, weight, preferred_element_type=jnp.float32) + bias
    return jax.nn.relu(projected).astype(jnp.bfloat16)


def solution(mesh):
    return jax.shard_map(
        layer,
        mesh=mesh,
        in_specs=(
            P(("row", "rep"), None),
            P(("row", "rep"), None, None),
            P(("row", "rep"), None),
            P(("row", "rep"), None),
            P(),
            P(),
            P(),
        ),
        out_specs=P(("row", "rep"), None),
        check_vma=False,
    )
```

profile of v0, /device:TPU:6, one launch (start us, length us, event | category | flops | bytes accessed | tf_op | source)
XLA Modules:
  0.0 57.6 jit_solution(2868907043278651694)
XLA Ops:
  0.0 0.0 copy-start
  0.0 1.9 %collective-permute-start = (bf16[128,128]{1,0:T(8,128)(2,1)}, bf16[128,128]{1,0:T(8,128)(2,1)S(1)}, u32[]{:S(2)}, u32[]{:S(2)}) collective-permute-start(bf16[128,128]{1,0:T(8,128)(2,1)} %param.7), channel_id=1, source_target_pairs={{0,128},{32,160},{64,192},{96,224},{128,0},{160,32},{192,64},{224,... | collective-permute-start | bytes 98312 | tf_op jit(solution)/shard_map/ppermute | solution.py:80
  1.9 0.8 %constant_dynamic-update-slice_fusion.4 = bf16[8,128,128]{2,1,0:T(8,128)(2,1)S(1)} fusion(bf16[128,128]{1,0:T(8,128)(2,1)} %param.7), kind=kLoop, calls=%fused_computation.54 | loop fusion | bytes 65536
  2.7 1.3 %dynamic_slice.41.count_ref = s32[1]{0:T(128)} dynamic-slice(s32[256]{0:T(256)} %param.11, s32[]{:T(128)S(6)} %select_n.81), dynamic_slice_sizes={1} | dynamic-slice | bytes 12 | tf_op jit(solution)/shard_map/dynamic_slice | solution.py:137
  4.0 0.2 collective-permute-done
  4.1 0.8 %pad_maximum_fusion = bf16[2,128,128]{2,1,0:T(8,128)(2,1)S(1)} fusion(bf16[1,128,128]{2,1,0:T(8,128)(2,1)S(1)} %bitcast.56, bf16[1,128,128]{2,1,0:T(8,128)(2,1)} %bitcast.55), kind=kLoop, calls=%fused_computation.49 | loop fusion | flops 32768 | bytes 131072 | tf_op jit(solution)/shard_map/stack | solution.py:81
  4.9 2.2 %collective-permute-start.1 = (bf16[2,128,128]{2,1,0:T(8,128)(2,1)S(1)}, bf16[2,128,128]{2,1,0:T(8,128)(2,1)S(1)}, u32[]{:S(2)}, u32[]{:S(2)}) collective-permute-start(bf16[2,128,128]{2,1,0:T(8,128)(2,1)S(1)} %pad_maximum_fusion), channel_id=1, source_target_pairs={{0,32},{32,64},{64,96},{96,0},{128,160},{160,192},{192,224},{224,1... | collective-permute-start | bytes 196616 | tf_op jit(solution)/shard_map/ppermute | solution.py:85
  7.1 0.7 %collective-permute-start.2 = (bf16[2,128,128]{2,1,0:T(8,128)(2,1)S(1)}, bf16[2,128,128]{2,1,0:T(8,128)(2,1)S(1)}, u32[]{:S(2)}, u32[]{:S(2)}) collective-permute-start(bf16[2,128,128]{2,1,0:T(8,128)(2,1)S(1)} %pad_maximum_fusion), channel_id=1, source_target_pairs={{0,64},{32,96},{64,0},{96,32},{128,192},{160,224},{192,128},{224,1... | collective-permute-start | bytes 196616 | tf_op jit(solution)/shard_map/ppermute | solution.py:85
  7.8 0.2 collective-permute-start.3
  8.0 1.6 %collective-permute-done.1 = bf16[2,128,128]{2,1,0:T(8,128)(2,1)S(1)} collective-permute-done((bf16[2,128,128]{2,1,0:T(8,128)(2,1)S(1)}, bf16[2,128,128]{2,1,0:T(8,128)(2,1)S(1)}, u32[]{:S(2)}, u32[]{:S(2)}) %collective-permute-start.1) | collective-permute-done | bytes 65568 | tf_op jit(solution)/shard_map/ppermute | solution.py:85
  9.6 3.3 %collective-permute-done.2 = bf16[2,128,128]{2,1,0:T(8,128)(2,1)S(1)} collective-permute-done((bf16[2,128,128]{2,1,0:T(8,128)(2,1)S(1)}, bf16[2,128,128]{2,1,0:T(8,128)(2,1)S(1)}, u32[]{:S(2)}, u32[]{:S(2)}) %collective-permute-start.2) | collective-permute-done | bytes 65568 | tf_op jit(solution)/shard_map/ppermute | solution.py:85
  12.9 0.7 %collective-permute-done.3 = bf16[2,128,128]{2,1,0:T(8,128)(2,1)S(1)} collective-permute-done((bf16[2,128,128]{2,1,0:T(8,128)(2,1)S(1)}, bf16[2,128,128]{2,1,0:T(8,128)(2,1)S(1)}, u32[]{:S(2)}, u32[]{:S(2)}) %collective-permute-start.3) | collective-permute-done | bytes 65568 | tf_op jit(solution)/shard_map/ppermute | solution.py:85
  13.6 0.0 copy-start.1
  13.6 0.7 %copy-done.1 = bf16[8,128,128]{2,1,0:T(8,128)(2,1)} copy-done((bf16[8,128,128]{2,1,0:T(8,128)(2,1)}, bf16[8,128,128]{2,1,0:T(8,128)(2,1)S(1)}, u32[]{:S(2)}) %copy-start.1) | copy-done | bytes 262168
  14.3 5.7 %shard_map.73 = (f32[16,128,128]{2,1,0:T(8,128)}, f32[16,128,128]{2,1,0:T(8,128)}) custom-call(s32[128]{0:T(128)} %bitcast.57, s32[128]{0:T(128)} %bitcast.58, s32[1]{0:T(128)} %dynamic_slice.41.count_ref, bf16[8,128,128]{2,1,0:T(8,128)(2,1)} %copy-done.1, bf16[128,128,128]{2,1,0:T(8,128)(2,1)} %vals_ref.1), custom_call_target="tpu_custom_call" | custom-call | flops 536870912 | bytes 6553600 | tf_op jit(solution)/shard_map/pallas_call | solution.py:64
  20.0 0.0 collective-permute-start.4
  20.0 2.9 %collective-permute-done.4 = f32[4,4,128,128]{3,2,1,0:T(8,128)S(1)} collective-permute-done((f32[4,4,128,128]{3,2,1,0:T(8,128)}, f32[4,4,128,128]{3,2,1,0:T(8,128)S(1)}, u32[]{:S(2)}, u32[]{:S(2)}) %collective-permute-start.4) | collective-permute-done | bytes 1048608 | tf_op jit(solution)/shard_map/ppermute | solution.py:104
  22.8 0.0 copy-start.2
  22.8 1.4 %add.127 = f32[4,4,128,128]{3,2,1,0:T(8,128)S(1)} add(f32[4,4,128,128]{3,2,1,0:T(8,128)} %bitcast.54, f32[4,4,128,128]{3,2,1,0:T(8,128)S(1)} %collective-permute-done.4) | non-fusion elementwise | flops 262144 | bytes 3145728 | tf_op jit(solution)/shard_map/add | solution.py:104
  24.2 0.1 constant_dynamic-slice_fusion
  24.3 2.8 %collective-permute-start.7 = (f32[2,128,128]{2,1,0:T(8,128)S(1)}, f32[2,128,128]{2,1,0:T(8,128)S(1)}, u32[]{:S(2)}, u32[]{:S(2)}) collective-permute-start(f32[2,128,128]{2,1,0:T(8,128)S(1)} %get-tuple-element.18), channel_id=1, source_target_pairs={{0,6},{1,7},{2,0},{3,1},{4,2},{5,3},{6,4},{7,5},{8,14},{9,15},{10,... | collective-permute-start | bytes 393224 | tf_op jit(solution)/shard_map/ppermute | solution.py:116
  27.2 0.6 %collective-permute-start.6 = (f32[2,128,128]{2,1,0:T(8,128)S(1)}, f32[2,128,128]{2,1,0:T(8,128)S(1)}, u32[]{:S(2)}, u32[]{:S(2)}) collective-permute-start(f32[2,128,128]{2,1,0:T(8,128)S(1)} %get-tuple-element.17), channel_id=1, source_target_pairs={{0,4},{1,5},{2,6},{3,7},{4,0},{5,1},{6,2},{7,3},{8,12},{9,13},{10,... | collective-permute-start | bytes 393224 | tf_op jit(solution)/shard_map/ppermute | solution.py:116
  27.8 1.0 %collective-permute-start.5 = (f32[2,128,128]{2,1,0:T(8,128)S(1)}, f32[2,128,128]{2,1,0:T(8,128)S(1)}, u32[]{:S(2)}, u32[]{:S(2)}) collective-permute-start(f32[2,128,128]{2,1,0:T(8,128)S(1)} %get-tuple-element.16), channel_id=1, source_target_pairs={{0,2},{1,3},{2,4},{3,5},{4,6},{5,7},{6,0},{7,1},{8,10},{9,11},{10,... | collective-permute-start | bytes 393224 | tf_op jit(solution)/shard_map/ppermute | solution.py:116
  28.8 2.3 %collective-permute-start.10 = (f32[2,128,128]{2,1,0:T(8,128)S(1)}, f32[2,128,128]{2,1,0:T(8,128)S(1)}, u32[]{:S(2)}, u32[]{:S(2)}) collective-permute-start(f32[2,128,128]{2,1,0:T(8,128)S(1)} %get-tuple-element.15), channel_id=1, source_target_pairs={{0,6},{1,7},{2,0},{3,1},{4,2},{5,3},{6,4},{7,5},{8,14},{9,15},{10,... | collective-permute-start | bytes 393224 | tf_op jit(solution)/shard_map/ppermute | solution.py:116
  31.1 1.7 %collective-permute-start.9 = (f32[2,128,128]{2,1,0:T(8,128)S(1)}, f32[2,128,128]{2,1,0:T(8,128)S(1)}, u32[]{:S(2)}, u32[]{:S(2)}) collective-permute-start(f32[2,128,128]{2,1,0:T(8,128)S(1)} %get-tuple-element.14), channel_id=1, source_target_pairs={{0,4},{1,5},{2,6},{3,7},{4,0},{5,1},{6,2},{7,3},{8,12},{9,13},{10,... | collective-permute-start | bytes 393224 | tf_op jit(solution)/shard_map/ppermute | solution.py:116
  32.8 0.8 %collective-permute-done.7 = f32[2,128,128]{2,1,0:T(8,128)S(1)} collective-permute-done((f32[2,128,128]{2,1,0:T(8,128)S(1)}, f32[2,128,128]{2,1,0:T(8,128)S(1)}, u32[]{:S(2)}, u32[]{:S(2)}) %collective-permute-start.7) | collective-permute-done | bytes 131104 | tf_op jit(solution)/shard_map/ppermute | solution.py:116
  33.7 0.0 collective-permute-start.8
  33.7 1.4 %collective-permute-done.6 = f32[2,128,128]{2,1,0:T(8,128)S(1)} collective-permute-done((f32[2,128,128]{2,1,0:T(8,128)S(1)}, f32[2,128,128]{2,1,0:T(8,128)S(1)}, u32[]{:S(2)}, u32[]{:S(2)}) %collective-permute-start.6) | collective-permute-done | bytes 131104 | tf_op jit(solution)/shard_map/ppermute | solution.py:116
  35.0 3.5 %collective-permute-done.5 = f32[2,128,128]{2,1,0:T(8,128)S(1)} collective-permute-done((f32[2,128,128]{2,1,0:T(8,128)S(1)}, f32[2,128,128]{2,1,0:T(8,128)S(1)}, u32[]{:S(2)}, u32[]{:S(2)}) %collective-permute-start.5) | collective-permute-done | bytes 131104 | tf_op jit(solution)/shard_map/ppermute | solution.py:116
  38.6 6.4 %collective-permute-start.13 = (f32[128,128]{1,0:T(8,128)S(1)}, f32[128,128]{1,0:T(8,128)S(1)}, u32[]{:S(2)}, u32[]{:S(2)}) collective-permute-start(f32[128,128]{1,0:T(8,128)S(1)} %slice_bitcast_fusion), channel_id=1, source_target_pairs={{0,24},{1,25},{2,26},{3,27},{4,28},{5,29},{6,30},{7,31},{8,0},{9,1... | collective-permute-start | bytes 196616 | tf_op jit(solution)/shard_map/ppermute | solution.py:129
  45.0 0.0 collective-permute-done.10
  45.0 0.0 collective-permute-done.9
  45.0 0.0 collective-permute-done.8
  45.1 4.6 %collective-permute-start.12 = (f32[128,128]{1,0:T(8,128)S(1)}, f32[128,128]{1,0:T(8,128)S(1)}, u32[]{:S(2)}, u32[]{:S(2)}) collective-permute-start(f32[128,128]{1,0:T(8,128)S(1)} %get-tuple-element.20), channel_id=1, source_target_pairs={{0,16},{1,17},{2,18},{3,19},{4,20},{5,21},{6,22},{7,23},{8,24},{9,... | collective-permute-start | bytes 196616 | tf_op jit(solution)/shard_map/ppermute | solution.py:129
  49.7 1.5 %collective-permute-start.11 = (f32[128,128]{1,0:T(8,128)S(1)}, f32[128,128]{1,0:T(8,128)S(1)}, u32[]{:S(2)}, u32[]{:S(2)}) collective-permute-start(f32[128,128]{1,0:T(8,128)S(1)} %get-tuple-element.19), channel_id=1, source_target_pairs={{0,8},{1,9},{2,10},{3,11},{4,12},{5,13},{6,14},{7,15},{8,16},{9,17... | collective-permute-start | bytes 196616 | tf_op jit(solution)/shard_map/ppermute | solution.py:129
  51.2 0.0 collective-permute-done.13
  51.2 2.3 %collective-permute-done.12 = f32[128,128]{1,0:T(8,128)S(1)} collective-permute-done((f32[128,128]{1,0:T(8,128)S(1)}, f32[128,128]{1,0:T(8,128)S(1)}, u32[]{:S(2)}, u32[]{:S(2)}) %collective-permute-start.12) | collective-permute-done | bytes 65568 | tf_op jit(solution)/shard_map/ppermute | solution.py:129
  53.4 3.4 %collective-permute-done.11 = f32[128,128]{1,0:T(8,128)S(1)} collective-permute-done((f32[128,128]{1,0:T(8,128)S(1)}, f32[128,128]{1,0:T(8,128)S(1)}, u32[]{:S(2)}, u32[]{:S(2)}) %collective-permute-start.11) | collective-permute-done | bytes 65568 | tf_op jit(solution)/shard_map/ppermute | solution.py:129
  56.8 0.0 copy-done
  56.8 0.0 copy-done.2
  56.9 0.8 %fusion.1 = bf16[128,256]{1,0:T(8,128)(2,1)} fusion(bf16[128,256]{1,0:T(8,128)(2,1)S(1)} %copy-done, f32[256]{0:T(256)S(1)} %copy-done.2, f32[128,128]{1,0:T(8,128)S(1)} %collective-permute-done.13, f32[128,128]{1,0:T(8,128)S(1)} %collective-permute-done.12, f32[128,128]{1,0:T(8,128)S(1)} %collective-permute-done.11, f32[2,128,128]{2,1,0:T(8,128)S(1)} %fusion.19), kind=kOutput, calls=%fused_computation.2 | convolution fusion | flops 8552448 | bytes 394240 | tf_op jit(solution)/shard_map/dot_general | solution.py:143
  (10 shorter events, 0.2 us)
Async XLA Ops:
  0.0 56.8 %copy-start = (bf16[128,256]{1,0:T(8,128)(2,1)S(1)}, bf16[128,256]{1,0:T(8,128)(2,1)}, u32[]{:S(2)}) copy-start(bf16[128,256]{1,0:T(8,128)(2,1)} %param.12) | copy-start | bytes 196612
  0.0 4.1 %collective-permute-start = (bf16[128,128]{1,0:T(8,128)(2,1)}, bf16[128,128]{1,0:T(8,128)(2,1)S(1)}, u32[]{:S(2)}, u32[]{:S(2)}) collective-permute-start(bf16[128,128]{1,0:T(8,128)(2,1)} %param.7), channel_id=1, source_target_pairs={{0,128},{32,160},{64,192},{96,224},{128,0},{160,32},{192,64},{224,... | collective-permute-start | bytes 98312 | tf_op jit(solution)/shard_map/ppermute | solution.py:80
  4.9 4.7 %collective-permute-start.1 = (bf16[2,128,128]{2,1,0:T(8,128)(2,1)S(1)}, bf16[2,128,128]{2,1,0:T(8,128)(2,1)S(1)}, u32[]{:S(2)}, u32[]{:S(2)}) collective-permute-start(bf16[2,128,128]{2,1,0:T(8,128)(2,1)S(1)} %pad_maximum_fusion), channel_id=1, source_target_pairs={{0,32},{32,64},{64,96},{96,0},{128,160},{160,192},{192,224},{224,1... | collective-permute-start | bytes 196616 | tf_op jit(solution)/shard_map/ppermute | solution.py:85
  7.1 5.8 %collective-permute-start.2 = (bf16[2,128,128]{2,1,0:T(8,128)(2,1)S(1)}, bf16[2,128,128]{2,1,0:T(8,128)(2,1)S(1)}, u32[]{:S(2)}, u32[]{:S(2)}) collective-permute-start(bf16[2,128,128]{2,1,0:T(8,128)(2,1)S(1)} %pad_maximum_fusion), channel_id=1, source_target_pairs={{0,64},{32,96},{64,0},{96,32},{128,192},{160,224},{192,128},{224,1... | collective-permute-start | bytes 196616 | tf_op jit(solution)/shard_map/ppermute | solution.py:85
  7.8 5.8 %collective-permute-start.3 = (bf16[2,128,128]{2,1,0:T(8,128)(2,1)S(1)}, bf16[2,128,128]{2,1,0:T(8,128)(2,1)S(1)}, u32[]{:S(2)}, u32[]{:S(2)}) collective-permute-start(bf16[2,128,128]{2,1,0:T(8,128)(2,1)S(1)} %pad_maximum_fusion), channel_id=1, source_target_pairs={{0,96},{32,0},{64,32},{96,64},{128,224},{160,128},{192,160},{224,1... | collective-permute-start | bytes 196616 | tf_op jit(solution)/shard_map/ppermute | solution.py:85
  13.6 0.7 %copy-start.1 = (bf16[8,128,128]{2,1,0:T(8,128)(2,1)}, bf16[8,128,128]{2,1,0:T(8,128)(2,1)S(1)}, u32[]{:S(2)}) copy-start(bf16[8,128,128]{2,1,0:T(8,128)(2,1)S(1)} %constant_dynamic-update-slice_fusion.feats_ref) | copy-start | bytes 786436
  20.0 2.9 %collective-permute-start.4 = (f32[4,4,128,128]{3,2,1,0:T(8,128)}, f32[4,4,128,128]{3,2,1,0:T(8,128)S(1)}, u32[]{:S(2)}, u32[]{:S(2)}) collective-permute-start(f32[4,4,128,128]{3,2,1,0:T(8,128)} %bitcast.59), channel_id=1, source_target_pairs={{0,1},{1,0},{2,3},{3,2},{4,5},{5,4},{6,7},{7,6},{8,9},{9,8},{10,11... | collective-permute-start | bytes 3145736 | tf_op jit(solution)/shard_map/ppermute | solution.py:104
  22.8 34.0 %copy-start.2 = (f32[256]{0:T(256)S(1)}, f32[256]{0:T(256)}, u32[]{:S(2)}) copy-start(f32[256]{0:T(256)} %param.13) | copy-start | bytes 3076
  24.3 9.3 %collective-permute-start.7 = (f32[2,128,128]{2,1,0:T(8,128)S(1)}, f32[2,128,128]{2,1,0:T(8,128)S(1)}, u32[]{:S(2)}, u32[]{:S(2)}) collective-permute-start(f32[2,128,128]{2,1,0:T(8,128)S(1)} %get-tuple-element.18), channel_id=1, source_target_pairs={{0,6},{1,7},{2,0},{3,1},{4,2},{5,3},{6,4},{7,5},{8,14},{9,15},{10,... | collective-permute-start | bytes 393224 | tf_op jit(solution)/shard_map/ppermute | solution.py:116
  27.2 7.9 %collective-permute-start.6 = (f32[2,128,128]{2,1,0:T(8,128)S(1)}, f32[2,128,128]{2,1,0:T(8,128)S(1)}, u32[]{:S(2)}, u32[]{:S(2)}) collective-permute-start(f32[2,128,128]{2,1,0:T(8,128)S(1)} %get-tuple-element.17), channel_id=1, source_target_pairs={{0,4},{1,5},{2,6},{3,7},{4,0},{5,1},{6,2},{7,3},{8,12},{9,13},{10,... | collective-permute-start | bytes 393224 | tf_op jit(solution)/shard_map/ppermute | solution.py:116
  27.8 10.8 %collective-permute-start.5 = (f32[2,128,128]{2,1,0:T(8,128)S(1)}, f32[2,128,128]{2,1,0:T(8,128)S(1)}, u32[]{:S(2)}, u32[]{:S(2)}) collective-permute-start(f32[2,128,128]{2,1,0:T(8,128)S(1)} %get-tuple-element.16), channel_id=1, source_target_pairs={{0,2},{1,3},{2,4},{3,5},{4,6},{5,7},{6,0},{7,1},{8,10},{9,11},{10,... | collective-permute-start | bytes 393224 | tf_op jit(solution)/shard_map/ppermute | solution.py:116
  28.8 16.2 %collective-permute-start.10 = (f32[2,128,128]{2,1,0:T(8,128)S(1)}, f32[2,128,128]{2,1,0:T(8,128)S(1)}, u32[]{:S(2)}, u32[]{:S(2)}) collective-permute-start(f32[2,128,128]{2,1,0:T(8,128)S(1)} %get-tuple-element.15), channel_id=1, source_target_pairs={{0,6},{1,7},{2,0},{3,1},{4,2},{5,3},{6,4},{7,5},{8,14},{9,15},{10,... | collective-permute-start | bytes 393224 | tf_op jit(solution)/shard_map/ppermute | solution.py:116
  31.1 13.9 %collective-permute-start.9 = (f32[2,128,128]{2,1,0:T(8,128)S(1)}, f32[2,128,128]{2,1,0:T(8,128)S(1)}, u32[]{:S(2)}, u32[]{:S(2)}) collective-permute-start(f32[2,128,128]{2,1,0:T(8,128)S(1)} %get-tuple-element.14), channel_id=1, source_target_pairs={{0,4},{1,5},{2,6},{3,7},{4,0},{5,1},{6,2},{7,3},{8,12},{9,13},{10,... | collective-permute-start | bytes 393224 | tf_op jit(solution)/shard_map/ppermute | solution.py:116
  33.7 11.4 %collective-permute-start.8 = (f32[2,128,128]{2,1,0:T(8,128)S(1)}, f32[2,128,128]{2,1,0:T(8,128)S(1)}, u32[]{:S(2)}, u32[]{:S(2)}) collective-permute-start(f32[2,128,128]{2,1,0:T(8,128)S(1)} %get-tuple-element.13), channel_id=1, source_target_pairs={{0,2},{1,3},{2,4},{3,5},{4,6},{5,7},{6,0},{7,1},{8,10},{9,11},{10,... | collective-permute-start | bytes 393224 | tf_op jit(solution)/shard_map/ppermute | solution.py:116
  38.6 12.5 %collective-permute-start.13 = (f32[128,128]{1,0:T(8,128)S(1)}, f32[128,128]{1,0:T(8,128)S(1)}, u32[]{:S(2)}, u32[]{:S(2)}) collective-permute-start(f32[128,128]{1,0:T(8,128)S(1)} %slice_bitcast_fusion), channel_id=1, source_target_pairs={{0,24},{1,25},{2,26},{3,27},{4,28},{5,29},{6,30},{7,31},{8,0},{9,1... | collective-permute-start | bytes 196616 | tf_op jit(solution)/shard_map/ppermute | solution.py:129
  45.1 8.3 %collective-permute-start.12 = (f32[128,128]{1,0:T(8,128)S(1)}, f32[128,128]{1,0:T(8,128)S(1)}, u32[]{:S(2)}, u32[]{:S(2)}) collective-permute-start(f32[128,128]{1,0:T(8,128)S(1)} %get-tuple-element.20), channel_id=1, source_target_pairs={{0,16},{1,17},{2,18},{3,19},{4,20},{5,21},{6,22},{7,23},{8,24},{9,... | collective-permute-start | bytes 196616 | tf_op jit(solution)/shard_map/ppermute | solution.py:129
  49.7 7.2 %collective-permute-start.11 = (f32[128,128]{1,0:T(8,128)S(1)}, f32[128,128]{1,0:T(8,128)S(1)}, u32[]{:S(2)}, u32[]{:S(2)}) collective-permute-start(f32[128,128]{1,0:T(8,128)S(1)} %get-tuple-element.19), channel_id=1, source_target_pairs={{0,8},{1,9},{2,10},{3,11},{4,12},{5,13},{6,14},{7,15},{8,16},{9,17... | collective-permute-start | bytes 196616 | tf_op jit(solution)/shard_map/ppermute | solution.py:129
where the time goes:
time: 57.9 us; the launch traced here: 57.6 us
  starting transfers between devices  25.9 us (45%)
  waiting for transfers between devices  20 us (35%)
  Pallas kernels  5.69 us (10%)
  local copies, waits for them, and re-layouts  2.92 us (5%)
  other arithmetic  2.26 us (4%)
  matrix products  0.79 us (1%)
    ppermute x3, starting transfers between devices, reduce_over_rep(): out = out + lax.ppermute(blocks[d], 'rep', z_pairs(rep_size, z_size, d))  12.4 us
    ppermute x6, starting transfers between devices, reduce_over_rep(): lax.ppermute(lax.dynamic_index_in_dim(part, (y + dy) % 4, 1, keepdims=Fal...  8.44 us
    ppermute x6, waiting for transfers between devices, reduce_over_rep(): lax.ppermute(lax.dynamic_index_in_dim(part, (y + dy) % 4, 1, keepdims=Fal...  5.77 us
    pallas_call x1, Pallas kernels, accumulate_slots(): pl.pallas_call(slot_kernel, grid_spec=grid_spec, out_shape=[half, half],...  5.69 us
    ppermute x3, waiting for transfers between devices, reduce_over_rep(): out = out + lax.ppermute(blocks[d], 'rep', z_pairs(rep_size, z_size, d))  5.69 us
    ppermute x3, waiting for transfers between devices, gather_over_row(): parts.append(lax.ppermute(pair, 'row', perm))  5.48 us
    ppermute x3, starting transfers between devices, gather_over_row(): parts.append(lax.ppermute(pair, 'row', perm))  3.14 us
    ppermute x1, waiting for transfers between devices, reduce_over_rep(): lax.ppermute(send.reshape(shape), 'rep', [(i, i ^ 1) for i in range(rep_s...  2.87 us
  transfers between devices with their start and end apart: 14, of which 10 were waited for; matrix products, arithmetic and copies ran while one was open for 4% of the time, Pallas kernels for 0%

commit v1 on v0

--- a/solution.py
+++ b/solution.py
@@ -101,16 +101,22 @@
     y = (j // 2) % 4
     z = j // 8
     shape = (z_size, 4) + keep.shape[1:]
-    x = keep.reshape(shape) + lax.ppermute(
-        send.reshape(shape), "rep", [(i, i ^ 1) for i in range(rep_size)]
-    )
+    keep = keep.reshape(shape)
+    send = send.reshape(shape)
     early = [d for d in range(1, z_size) if d < z_size - 1]
     late = [0] + [d for d in range(1, z_size) if d not in early]
     blocks = {}
     for shifts in (early, late):
+        got = lax.ppermute(
+            jnp.stack(
+                [lax.dynamic_index_in_dim(send, (z + d) % z_size, 0, keepdims=False) for d in shifts]
+            ),
+            "rep",
+            [(i, i ^ 1) for i in range(rep_size)],
+        )
         part = jnp.stack(
-            [lax.dynamic_index_in_dim(x, (z + d) % z_size, 0, keepdims=False) for d in shifts]
-        )
+            [lax.dynamic_index_in_dim(keep, (z + d) % z_size, 0, keepdims=False) for d in shifts]
+        ) + got
         acc = lax.dynamic_index_in_dim(part, y, 1, keepdims=False)
         got = [
             lax.ppermute(

time: 57.9 us -> 51.1 us (0.88)
  waiting for transfers between devices: 20 us -> 10.6 us
  starting transfers between devices: 25.9 us -> 27.8 us
  local copies, waits for them, and re-layouts: 2.92 us -> 4.33 us
  other arithmetic: 2.26 us -> 1.01 us
    ppermute x6, waiting for transfers between devices: 5.77 us -> 0.96 us  [reduce_over_rep(): lax.ppermute(lax.dynamic_index_in_dim(part, (y + dy) % 4, 1, keepdims=Fal...]
    ppermute x3, waiting for transfers between devices: 5.69 us -> 2.77 us  [reduce_over_rep(): out = out + lax.ppermute(blocks[d], 'rep', z_pairs(rep_size, z_size, d))]
    ppermute x6, starting transfers between devices: 8.44 us -> 10.6 us  [reduce_over_rep(): lax.ppermute(lax.dynamic_index_in_dim(part, (y + dy) % 4, 1, keepdims=Fal...]
    ppermute x1 -> x2, waiting for transfers between devices: 2.87 us -> 1.2 us  [reduce_over_rep(): lax.ppermute(jnp.stack([lax.dynamic_index_in_dim(send, (z + d) % z_size,...]
    dynamic_slice x1 -> x2, local copies, waits for them, and re-layouts: 0.1 us -> 1.44 us  [the longest x1 1.37 us: reduce_over_rep(): lax.dynamic_index_in_dim(send, (z + d) % z_size, 0, keepdims=False)]
    add x1 -> x2, other arithmetic: 1.35 us -> 0.11 us  [reduce_over_rep(): jnp.stack([lax.dynamic_index_in_dim(keep, (z + d) % z_size, 0, keepdims=F...]
    ppermute x3, starting transfers between devices: 12.4 us -> 11.5 us  [reduce_over_rep(): out = out + lax.ppermute(blocks[d], 'rep', z_pairs(rep_size, z_size, d))]
    ppermute x1 -> x2, starting transfers between devices: 0.01 us -> 0.67 us  [reduce_over_rep(): lax.ppermute(jnp.stack([lax.dynamic_index_in_dim(send, (z + d) % z_size,...]
  transfers between devices with their start and end apart: 14 -> 15, of which waited for: 10 -> 9; matrix products, arithmetic and copies ran while one was open for 4% -> 5% of each run, Pallas kernels for 0% -> 0%
where the time goes in v1:
time: 51.1 us; the launch traced here: 50.3 us
  starting transfers between devices  27.8 us (54%)
  waiting for transfers between devices  10.6 us (21%)
  Pallas kernels  5.7 us (11%)
  local copies, waits for them, and re-layouts  4.33 us (8%)
  other arithmetic  1.01 us (2%)
  matrix products  0.78 us (2%)
    ppermute x3, starting transfers between devices, reduce_over_rep(): out = out + lax.ppermute(blocks[d], 'rep', z_pairs(rep_size, z_size, d))  11.5 us
    ppermute x6, starting transfers between devices, reduce_over_rep(): lax.ppermute(lax.dynamic_index_in_dim(part, (y + dy) % 4, 1, keepdims=Fal...  10.6 us
    pallas_call x1, Pallas kernels, accumulate_slots(): pl.pallas_call(slot_kernel, grid_spec=grid_spec, out_shape=[half, half],...  5.7 us
    ppermute x3, waiting for transfers between devices, gather_over_row(): parts.append(lax.ppermute(pair, 'row', perm))  5.48 us
    ppermute x3, starting transfers between devices, gather_over_row(): parts.append(lax.ppermute(pair, 'row', perm))  3.14 us
    ppermute x3, waiting for transfers between devices, reduce_over_rep(): out = out + lax.ppermute(blocks[d], 'rep', z_pairs(rep_size, z_size, d))  2.77 us
    ppermute x1, starting transfers between devices, gather_over_row(): lax.ppermute(x, 'row', [(s, (s + x_size) % row_size) for s in range(row_s...  1.92 us
    unnamed x12, local copies, waits for them, and re-layouts  1.53 us
  transfers between devices with their start and end apart: 15, of which 9 were waited for; matrix products, arithmetic and copies ran while one was open for 5% of the time, Pallas kernels for 0%

profile of v1, /device:TPU:6, one launch (start us, length us, event | category | flops | bytes accessed | tf_op | source)
XLA Modules:
  0.0 50.3 jit_solution(13943555754110213792)
XLA Ops:
  0.0 0.0 copy-start
  0.0 1.9 %collective-permute-start = (bf16[128,128]{1,0:T(8,128)(2,1)}, bf16[128,128]{1,0:T(8,128)(2,1)S(1)}, u32[]{:S(2)}, u32[]{:S(2)}) collective-permute-start(bf16[128,128]{1,0:T(8,128)(2,1)} %param.7), channel_id=1, source_target_pairs={{0,128},{32,160},{64,192},{96,224},{128,0},{160,32},{192,64},{224,... | collective-permute-start | bytes 98312 | tf_op jit(solution)/shard_map/ppermute | solution.py:80
  1.9 0.8 %constant_dynamic-update-slice_fusion.4 = bf16[8,128,128]{2,1,0:T(8,128)(2,1)S(1)} fusion(bf16[128,128]{1,0:T(8,128)(2,1)} %param.7), kind=kLoop, calls=%fused_computation.32 | loop fusion | bytes 65536
  2.7 1.3 %dynamic_slice.53.count_ref = s32[1]{0:T(128)} dynamic-slice(s32[256]{0:T(256)} %param.11, s32[]{:T(128)S(6)} %select_n.93), dynamic_slice_sizes={1} | dynamic-slice | bytes 12 | tf_op jit(solution)/shard_map/dynamic_slice | solution.py:143
  4.0 0.2 collective-permute-done
  4.1 0.8 %pad_maximum_fusion.2 = bf16[2,128,128]{2,1,0:T(8,128)(2,1)S(1)} fusion(bf16[1,128,128]{2,1,0:T(8,128)(2,1)S(1)} %bitcast.53, bf16[1,128,128]{2,1,0:T(8,128)(2,1)} %bitcast.52), kind=kLoop, calls=%fused_computation.27 | loop fusion | flops 32768 | bytes 131072 | tf_op jit(solution)/shard_map/stack | solution.py:81
  4.9 2.2 %collective-permute-start.1 = (bf16[2,128,128]{2,1,0:T(8,128)(2,1)S(1)}, bf16[2,128,128]{2,1,0:T(8,128)(2,1)S(1)}, u32[]{:S(2)}, u32[]{:S(2)}) collective-permute-start(bf16[2,128,128]{2,1,0:T(8,128)(2,1)S(1)} %pad_maximum_fusion.2), channel_id=1, source_target_pairs={{0,32},{32,64},{64,96},{96,0},{128,160},{160,192},{192,224},{224,1... | collective-permute-start | bytes 196616 | tf_op jit(solution)/shard_map/ppermute | solution.py:85
  7.1 0.7 %collective-permute-start.2 = (bf16[2,128,128]{2,1,0:T(8,128)(2,1)S(1)}, bf16[2,128,128]{2,1,0:T(8,128)(2,1)S(1)}, u32[]{:S(2)}, u32[]{:S(2)}) collective-permute-start(bf16[2,128,128]{2,1,0:T(8,128)(2,1)S(1)} %pad_maximum_fusion.2), channel_id=1, source_target_pairs={{0,64},{32,96},{64,0},{96,32},{128,192},{160,224},{192,128},{224,1... | collective-permute-start | bytes 196616 | tf_op jit(solution)/shard_map/ppermute | solution.py:85
  7.8 0.2 collective-permute-start.3
  8.0 1.6 %collective-permute-done.1 = bf16[2,128,128]{2,1,0:T(8,128)(2,1)S(1)} collective-permute-done((bf16[2,128,128]{2,1,0:T(8,128)(2,1)S(1)}, bf16[2,128,128]{2,1,0:T(8,128)(2,1)S(1)}, u32[]{:S(2)}, u32[]{:S(2)}) %collective-permute-start.1) | collective-permute-done | bytes 65568 | tf_op jit(solution)/shard_map/ppermute | solution.py:85
  9.6 3.3 %collective-permute-done.2 = bf16[2,128,128]{2,1,0:T(8,128)(2,1)S(1)} collective-permute-done((bf16[2,128,128]{2,1,0:T(8,128)(2,1)S(1)}, bf16[2,128,128]{2,1,0:T(8,128)(2,1)S(1)}, u32[]{:S(2)}, u32[]{:S(2)}) %collective-permute-start.2) | collective-permute-done | bytes 65568 | tf_op jit(solution)/shard_map/ppermute | solution.py:85
  12.9 0.7 %collective-permute-done.3 = bf16[2,128,128]{2,1,0:T(8,128)(2,1)S(1)} collective-permute-done((bf16[2,128,128]{2,1,0:T(8,128)(2,1)S(1)}, bf16[2,128,128]{2,1,0:T(8,128)(2,1)S(1)}, u32[]{:S(2)}, u32[]{:S(2)}) %collective-permute-start.3) | collective-permute-done | bytes 65568 | tf_op jit(solution)/shard_map/ppermute | solution.py:85
  13.6 0.0 copy-start.2
  13.6 0.7 %copy-done.2 = bf16[8,128,128]{2,1,0:T(8,128)(2,1)} copy-done((bf16[8,128,128]{2,1,0:T(8,128)(2,1)}, bf16[8,128,128]{2,1,0:T(8,128)(2,1)S(1)}, u32[]{:S(2)}) %copy-start.2) | copy-done | bytes 262168
  14.3 5.7 %shard_map.73 = (f32[16,128,128]{2,1,0:T(8,128)}, f32[16,128,128]{2,1,0:T(8,128)}) custom-call(s32[128]{0:T(128)} %bitcast.54, s32[128]{0:T(128)} %bitcast.55, s32[1]{0:T(128)} %dynamic_slice.53.count_ref, bf16[8,128,128]{2,1,0:T(8,128)(2,1)} %copy-done.2, bf16[128,128,128]{2,1,0:T(8,128)(2,1)} %vals_ref.1), custom_call_target="tpu_custom_call" | custom-call | flops 536870912 | bytes 6553600 | tf_op jit(solution)/shard_map/pallas_call | solution.py:64
  20.0 0.0 copy-start.1
  20.0 1.4 %constant_dynamic-slice_fusion.1 = (f32[1,4,128,128]{3,2,1,0:T(8,128)S(1)}, f32[1,4,128,128]{3,2,1,0:T(8,128)S(1)}, f32[1,4,128,128]{3,2,1,0:T(8,128)S(1)}, f32[1,4,128,128]{3,2,1,0:T(8,128)S(1)}) fusion(f32[4,4,128,128]{3,2,1,0:T(8,128)} %bitcast.51, s32[]{:T(128)S(6)} %select_n.109, s32[]{:T(128)S(6)} %select_n.111, s32[]{:T(128)S(6)} %select_n.98, ...), kind=kLoop, calls=%fused_computation.34 | loop fusion | bytes 2097168 | tf_op jit(solution)/shard_map/jit(dynamic_index_in_dim)/dynamic_slice | solution.py:112
  21.4 0.1 collective-permute-start.8
  21.5 0.6 %collective-permute-start.4 = (f32[2,4,128,128]{3,2,1,0:T(8,128)S(1)}, f32[2,4,128,128]{3,2,1,0:T(8,128)S(1)}, u32[]{:S(2)}, u32[]{:S(2)}) collective-permute-start(f32[2,4,128,128]{3,2,1,0:T(8,128)S(1)} %pad_maximum_fusion), channel_id=1, source_target_pairs={{0,1},{1,0},{2,3},{3,2},{4,5},{5,4},{6,7},{7,6},{8,9},{9,8},{10,11... | collective-permute-start | bytes 1572872 | tf_op jit(solution)/shard_map/ppermute | solution.py:110
  22.1 0.0 copy-done.1
  22.1 0.0 copy-start.3
  22.1 0.1 constant_dynamic-slice_fusion.3
  22.2 1.2 %collective-permute-done.8 = f32[2,4,128,128]{3,2,1,0:T(8,128)S(1)} collective-permute-done((f32[2,4,128,128]{3,2,1,0:T(8,128)S(1)}, f32[2,4,128,128]{3,2,1,0:T(8,128)S(1)}, u32[]{:S(2)}, u32[]{:S(2)}) %collective-permute-start.8) | collective-permute-done | bytes 524320 | tf_op jit(solution)/shard_map/ppermute | solution.py:110
  23.4 0.1 maximum_add_fusion.1
  23.5 3.0 %collective-permute-start.10 = (f32[2,128,128]{2,1,0:T(8,128)S(1)}, f32[2,128,128]{2,1,0:T(8,128)S(1)}, u32[]{:S(2)}, u32[]{:S(2)}) collective-permute-start(f32[2,128,128]{2,1,0:T(8,128)S(1)} %get-tuple-element.19), channel_id=1, source_target_pairs={{0,4},{1,5},{2,6},{3,7},{4,0},{5,1},{6,2},{7,3},{8,12},{9,13},{10,... | collective-permute-start | bytes 393224 | tf_op jit(solution)/shard_map/ppermute | solution.py:122
  26.5 1.1 %collective-permute-start.11 = (f32[2,128,128]{2,1,0:T(8,128)S(1)}, f32[2,128,128]{2,1,0:T(8,128)S(1)}, u32[]{:S(2)}, u32[]{:S(2)}) collective-permute-start(f32[2,128,128]{2,1,0:T(8,128)S(1)} %get-tuple-element.18), channel_id=1, source_target_pairs={{0,6},{1,7},{2,0},{3,1},{4,2},{5,3},{6,4},{7,5},{8,14},{9,15},{10,... | collective-permute-start | bytes 393224 | tf_op jit(solution)/shard_map/ppermute | solution.py:122
  27.5 1.0 %collective-permute-start.9 = (f32[2,128,128]{2,1,0:T(8,128)S(1)}, f32[2,128,128]{2,1,0:T(8,128)S(1)}, u32[]{:S(2)}, u32[]{:S(2)}) collective-permute-start(f32[2,128,128]{2,1,0:T(8,128)S(1)} %get-tuple-element.17), channel_id=1, source_target_pairs={{0,2},{1,3},{2,4},{3,5},{4,6},{5,7},{6,0},{7,1},{8,10},{9,11},{10,... | collective-permute-start | bytes 393224 | tf_op jit(solution)/shard_map/ppermute | solution.py:122
  28.5 0.0 collective-permute-done.4
  28.5 0.1 maximum_add_fusion
  28.6 0.8 %collective-permute-start.5 = (f32[2,128,128]{2,1,0:T(8,128)S(1)}, f32[2,128,128]{2,1,0:T(8,128)S(1)}, u32[]{:S(2)}, u32[]{:S(2)}) collective-permute-start(f32[2,128,128]{2,1,0:T(8,128)S(1)} %get-tuple-element.20), channel_id=1, source_target_pairs={{0,2},{1,3},{2,4},{3,5},{4,6},{5,7},{6,0},{7,1},{8,10},{9,11},{10,... | collective-permute-start | bytes 393224 | tf_op jit(solution)/shard_map/ppermute | solution.py:122
  29.4 3.1 %collective-permute-start.6 = (f32[2,128,128]{2,1,0:T(8,128)S(1)}, f32[2,128,128]{2,1,0:T(8,128)S(1)}, u32[]{:S(2)}, u32[]{:S(2)}) collective-permute-start(f32[2,128,128]{2,1,0:T(8,128)S(1)} %get-tuple-element.22), channel_id=1, source_target_pairs={{0,4},{1,5},{2,6},{3,7},{4,0},{5,1},{6,2},{7,3},{8,12},{9,13},{10,... | collective-permute-start | bytes 393224 | tf_op jit(solution)/shard_map/ppermute | solution.py:122
  32.4 0.0 collective-permute-done.10
  32.4 1.7 %collective-permute-start.7 = (f32[2,128,128]{2,1,0:T(8,128)S(1)}, f32[2,128,128]{2,1,0:T(8,128)S(1)}, u32[]{:S(2)}, u32[]{:S(2)}) collective-permute-start(f32[2,128,128]{2,1,0:T(8,128)S(1)} %get-tuple-element.21), channel_id=1, source_target_pairs={{0,6},{1,7},{2,0},{3,1},{4,2},{5,3},{6,4},{7,5},{8,14},{9,15},{10,... | collective-permute-start | bytes 393224 | tf_op jit(solution)/shard_map/ppermute | solution.py:122
  34.2 0.1 collective-permute-done.11
  34.3 0.8 %collective-permute-done.9 = f32[2,128,128]{2,1,0:T(8,128)S(1)} collective-permute-done((f32[2,128,128]{2,1,0:T(8,128)S(1)}, f32[2,128,128]{2,1,0:T(8,128)S(1)}, u32[]{:S(2)}, u32[]{:S(2)}) %collective-permute-start.9) | collective-permute-done | bytes 131104 | tf_op jit(solution)/shard_map/ppermute | solution.py:122
  35.2 3.3 %collective-permute-start.12 = (f32[128,128]{1,0:T(8,128)S(1)}, f32[128,128]{1,0:T(8,128)S(1)}, u32[]{:S(2)}, u32[]{:S(2)}) collective-permute-start(f32[128,128]{1,0:T(8,128)S(1)} %get-tuple-element.23), channel_id=1, source_target_pairs={{0,8},{1,9},{2,10},{3,11},{4,12},{5,13},{6,14},{7,15},{8,16},{9,17... | collective-permute-start | bytes 196616 | tf_op jit(solution)/shard_map/ppermute | solution.py:135
  38.5 5.4 %collective-permute-start.13 = (f32[128,128]{1,0:T(8,128)S(1)}, f32[128,128]{1,0:T(8,128)S(1)}, u32[]{:S(2)}, u32[]{:S(2)}) collective-permute-start(f32[128,128]{1,0:T(8,128)S(1)} %get-tuple-element.24), channel_id=1, source_target_pairs={{0,16},{1,17},{2,18},{3,19},{4,20},{5,21},{6,22},{7,23},{8,24},{9,... | collective-permute-start | bytes 196616 | tf_op jit(solution)/shard_map/ppermute | solution.py:135
  43.9 0.0 collective-permute-done.5
  43.9 0.0 collective-permute-done.6
  43.9 0.0 collective-permute-done.7
  44.0 2.7 %collective-permute-start.14 = (f32[128,128]{1,0:T(8,128)S(1)}, f32[128,128]{1,0:T(8,128)S(1)}, u32[]{:S(2)}, u32[]{:S(2)}) collective-permute-start(f32[128,128]{1,0:T(8,128)S(1)} %slice_bitcast_fusion), channel_id=1, source_target_pairs={{0,24},{1,25},{2,26},{3,27},{4,28},{5,29},{6,30},{7,31},{8,0},{9,1... | collective-permute-start | bytes 196616 | tf_op jit(solution)/shard_map/ppermute | solution.py:135
  46.7 0.0 collective-permute-done.12
  46.7 0.9 %collective-permute-done.13 = f32[128,128]{1,0:T(8,128)S(1)} collective-permute-done((f32[128,128]{1,0:T(8,128)S(1)}, f32[128,128]{1,0:T(8,128)S(1)}, u32[]{:S(2)}, u32[]{:S(2)}) %collective-permute-start.13) | collective-permute-done | bytes 65568 | tf_op jit(solution)/shard_map/ppermute | solution.py:135
  47.6 1.9 %collective-permute-done.14 = f32[128,128]{1,0:T(8,128)S(1)} collective-permute-done((f32[128,128]{1,0:T(8,128)S(1)}, f32[128,128]{1,0:T(8,128)S(1)}, u32[]{:S(2)}, u32[]{:S(2)}) %collective-permute-start.14) | collective-permute-done | bytes 65568 | tf_op jit(solution)/shard_map/ppermute | solution.py:135
  49.5 0.0 copy-done
  49.5 0.0 copy-done.3
  49.5 0.8 %fusion.1 = bf16[128,256]{1,0:T(8,128)(2,1)} fusion(bf16[128,256]{1,0:T(8,128)(2,1)S(1)} %copy-done, f32[256]{0:T(256)S(1)} %copy-done.3, f32[128,128]{1,0:T(8,128)S(1)} %collective-permute-done.14, f32[128,128]{1,0:T(8,128)S(1)} %collective-permute-done.13, f32[128,128]{1,0:T(8,128)S(1)} %collective-permute-done.12, f32[2,128,128]{2,1,0:T(8,128)S(1)} %fusion.5), kind=kOutput, calls=%fused_computation.2 | convolution fusion | flops 8552448 | bytes 394240 | tf_op jit(solution)/shard_map/dot_general | solution.py:149
  (12 shorter events, 0.3 us)
Async XLA Ops:
  0.0 49.5 %copy-start = (bf16[128,256]{1,0:T(8,128)(2,1)S(1)}, bf16[128,256]{1,0:T(8,128)(2,1)}, u32[]{:S(2)}) copy-start(bf16[128,256]{1,0:T(8,128)(2,1)} %param.12) | copy-start | bytes 196612
  0.0 4.1 %collective-permute-start = (bf16[128,128]{1,0:T(8,128)(2,1)}, bf16[128,128]{1,0:T(8,128)(2,1)S(1)}, u32[]{:S(2)}, u32[]{:S(2)}) collective-permute-start(bf16[128,128]{1,0:T(8,128)(2,1)} %param.7), channel_id=1, source_target_pairs={{0,128},{32,160},{64,192},{96,224},{128,0},{160,32},{192,64},{224,... | collective-permute-start | bytes 98312 | tf_op jit(solution)/shard_map/ppermute | solution.py:80
  4.9 4.7 %collective-permute-start.1 = (bf16[2,128,128]{2,1,0:T(8,128)(2,1)S(1)}, bf16[2,128,128]{2,1,0:T(8,128)(2,1)S(1)}, u32[]{:S(2)}, u32[]{:S(2)}) collective-permute-start(bf16[2,128,128]{2,1,0:T(8,128)(2,1)S(1)} %pad_maximum_fusion.2), channel_id=1, source_target_pairs={{0,32},{32,64},{64,96},{96,0},{128,160},{160,192},{192,224},{224,1... | collective-permute-start | bytes 196616 | tf_op jit(solution)/shard_map/ppermute | solution.py:85
  7.1 5.8 %collective-permute-start.2 = (bf16[2,128,128]{2,1,0:T(8,128)(2,1)S(1)}, bf16[2,128,128]{2,1,0:T(8,128)(2,1)S(1)}, u32[]{:S(2)}, u32[]{:S(2)}) collective-permute-start(bf16[2,128,128]{2,1,0:T(8,128)(2,1)S(1)} %pad_maximum_fusion.2), channel_id=1, source_target_pairs={{0,64},{32,96},{64,0},{96,32},{128,192},{160,224},{192,128},{224,1... | collective-permute-start | bytes 196616 | tf_op jit(solution)/shard_map/ppermute | solution.py:85
  7.8 5.8 %collective-permute-start.3 = (bf16[2,128,128]{2,1,0:T(8,128)(2,1)S(1)}, bf16[2,128,128]{2,1,0:T(8,128)(2,1)S(1)}, u32[]{:S(2)}, u32[]{:S(2)}) collective-permute-start(bf16[2,128,128]{2,1,0:T(8,128)(2,1)S(1)} %pad_maximum_fusion.2), channel_id=1, source_target_pairs={{0,96},{32,0},{64,32},{96,64},{128,224},{160,128},{192,160},{224,1... | collective-permute-start | bytes 196616 | tf_op jit(solution)/shard_map/ppermute | solution.py:85
  13.6 0.7 %copy-start.2 = (bf16[8,128,128]{2,1,0:T(8,128)(2,1)}, bf16[8,128,128]{2,1,0:T(8,128)(2,1)S(1)}, u32[]{:S(2)}) copy-start(bf16[8,128,128]{2,1,0:T(8,128)(2,1)S(1)} %constant_dynamic-update-slice_fusion.feats_ref) | copy-start | bytes 786436
  20.0 2.1 %copy-start.1 = (f32[16,128,128]{2,1,0:T(8,128)S(1)}, f32[16,128,128]{2,1,0:T(8,128)}, u32[]{:S(2)}) copy-start(f32[16,128,128]{2,1,0:T(8,128)} %get-tuple-element.7) | copy-start | bytes 3145732
  21.4 2.0 %collective-permute-start.8 = (f32[2,4,128,128]{3,2,1,0:T(8,128)S(1)}, f32[2,4,128,128]{3,2,1,0:T(8,128)S(1)}, u32[]{:S(2)}, u32[]{:S(2)}) collective-permute-start(f32[2,4,128,128]{3,2,1,0:T(8,128)S(1)} %pad_maximum_fusion.1), channel_id=1, source_target_pairs={{0,1},{1,0},{2,3},{3,2},{4,5},{5,4},{6,7},{7,6},{8,9},{9,8},{10,11... | collective-permute-start | bytes 1572872 | tf_op jit(solution)/shard_map/ppermute | solution.py:110
  21.5 7.0 %collective-permute-start.4 = (f32[2,4,128,128]{3,2,1,0:T(8,128)S(1)}, f32[2,4,128,128]{3,2,1,0:T(8,128)S(1)}, u32[]{:S(2)}, u32[]{:S(2)}) collective-permute-start(f32[2,4,128,128]{3,2,1,0:T(8,128)S(1)} %pad_maximum_fusion), channel_id=1, source_target_pairs={{0,1},{1,0},{2,3},{3,2},{4,5},{5,4},{6,7},{7,6},{8,9},{9,8},{10,11... | collective-permute-start | bytes 1572872 | tf_op jit(solution)/shard_map/ppermute | solution.py:110
  22.1 27.4 %copy-start.3 = (f32[256]{0:T(256)S(1)}, f32[256]{0:T(256)}, u32[]{:S(2)}) copy-start(f32[256]{0:T(256)} %param.13) | copy-start | bytes 3076
  23.5 8.9 %collective-permute-start.10 = (f32[2,128,128]{2,1,0:T(8,128)S(1)}, f32[2,128,128]{2,1,0:T(8,128)S(1)}, u32[]{:S(2)}, u32[]{:S(2)}) collective-permute-start(f32[2,128,128]{2,1,0:T(8,128)S(1)} %get-tuple-element.19), channel_id=1, source_target_pairs={{0,4},{1,5},{2,6},{3,7},{4,0},{5,1},{6,2},{7,3},{8,12},{9,13},{10,... | collective-permute-start | bytes 393224 | tf_op jit(solution)/shard_map/ppermute | solution.py:122
  26.5 7.8 %collective-permute-start.11 = (f32[2,128,128]{2,1,0:T(8,128)S(1)}, f32[2,128,128]{2,1,0:T(8,128)S(1)}, u32[]{:S(2)}, u32[]{:S(2)}) collective-permute-start(f32[2,128,128]{2,1,0:T(8,128)S(1)} %get-tuple-element.18), channel_id=1, source_target_pairs={{0,6},{1,7},{2,0},{3,1},{4,2},{5,3},{6,4},{7,5},{8,14},{9,15},{10,... | collective-permute-start | bytes 393224 | tf_op jit(solution)/shard_map/ppermute | solution.py:122
  27.5 7.6 %collective-permute-start.9 = (f32[2,128,128]{2,1,0:T(8,128)S(1)}, f32[2,128,128]{2,1,0:T(8,128)S(1)}, u32[]{:S(2)}, u32[]{:S(2)}) collective-permute-start(f32[2,128,128]{2,1,0:T(8,128)S(1)} %get-tuple-element.17), channel_id=1, source_target_pairs={{0,2},{1,3},{2,4},{3,5},{4,6},{5,7},{6,0},{7,1},{8,10},{9,11},{10,... | collective-permute-start | bytes 393224 | tf_op jit(solution)/shard_map/ppermute | solution.py:122
  28.6 15.3 %collective-permute-start.5 = (f32[2,128,128]{2,1,0:T(8,128)S(1)}, f32[2,128,128]{2,1,0:T(8,128)S(1)}, u32[]{:S(2)}, u32[]{:S(2)}) collective-permute-start(f32[2,128,128]{2,1,0:T(8,128)S(1)} %get-tuple-element.20), channel_id=1, source_target_pairs={{0,2},{1,3},{2,4},{3,5},{4,6},{5,7},{6,0},{7,1},{8,10},{9,11},{10,... | collective-permute-start | bytes 393224 | tf_op jit(solution)/shard_map/ppermute | solution.py:122
  29.4 14.5 %collective-permute-start.6 = (f32[2,128,128]{2,1,0:T(8,128)S(1)}, f32[2,128,128]{2,1,0:T(8,128)S(1)}, u32[]{:S(2)}, u32[]{:S(2)}) collective-permute-start(f32[2,128,128]{2,1,0:T(8,128)S(1)} %get-tuple-element.22), channel_id=1, source_target_pairs={{0,4},{1,5},{2,6},{3,7},{4,0},{5,1},{6,2},{7,3},{8,12},{9,13},{10,... | collective-permute-start | bytes 393224 | tf_op jit(solution)/shard_map/ppermute | solution.py:122
  32.4 11.5 %collective-permute-start.7 = (f32[2,128,128]{2,1,0:T(8,128)S(1)}, f32[2,128,128]{2,1,0:T(8,128)S(1)}, u32[]{:S(2)}, u32[]{:S(2)}) collective-permute-start(f32[2,128,128]{2,1,0:T(8,128)S(1)} %get-tuple-element.21), channel_id=1, source_target_pairs={{0,6},{1,7},{2,0},{3,1},{4,2},{5,3},{6,4},{7,5},{8,14},{9,15},{10,... | collective-permute-start | bytes 393224 | tf_op jit(solution)/shard_map/ppermute | solution.py:122
  35.2 11.6 %collective-permute-start.12 = (f32[128,128]{1,0:T(8,128)S(1)}, f32[128,128]{1,0:T(8,128)S(1)}, u32[]{:S(2)}, u32[]{:S(2)}) collective-permute-start(f32[128,128]{1,0:T(8,128)S(1)} %get-tuple-element.23), channel_id=1, source_target_pairs={{0,8},{1,9},{2,10},{3,11},{4,12},{5,13},{6,14},{7,15},{8,16},{9,17... | collective-permute-start | bytes 196616 | tf_op jit(solution)/shard_map/ppermute | solution.py:135
  38.5 9.1 %collective-permute-start.13 = (f32[128,128]{1,0:T(8,128)S(1)}, f32[128,128]{1,0:T(8,128)S(1)}, u32[]{:S(2)}, u32[]{:S(2)}) collective-permute-start(f32[128,128]{1,0:T(8,128)S(1)} %get-tuple-element.24), channel_id=1, source_target_pairs={{0,16},{1,17},{2,18},{3,19},{4,20},{5,21},{6,22},{7,23},{8,24},{9,... | collective-permute-start | bytes 196616 | tf_op jit(solution)/shard_map/ppermute | solution.py:135
  44.0 5.5 %collective-permute-start.14 = (f32[128,128]{1,0:T(8,128)S(1)}, f32[128,128]{1,0:T(8,128)S(1)}, u32[]{:S(2)}, u32[]{:S(2)}) collective-permute-start(f32[128,128]{1,0:T(8,128)S(1)} %slice_bitcast_fusion), channel_id=1, source_target_pairs={{0,24},{1,25},{2,26},{3,27},{4,28},{5,29},{6,30},{7,31},{8,0},{9,1... | collective-permute-start | bytes 196616 | tf_op jit(solution)/shard_map/ppermute | solution.py:135

commit v2 on v1

--- a/solution.py
+++ b/solution.py
@@ -77,12 +77,15 @@
 def gather_over_row(x):
     row_size = lax.axis_size("row")
     x_size = row_size // 2
+
+    def shift(d):
+        return [(s, (s // x_size) * x_size + (s % x_size + d) % x_size) for s in range(row_size)]
+
+    own = [lax.ppermute(x, "row", shift(d)) for d in range(1, x_size)]
     other = lax.ppermute(x, "row", [(s, (s + x_size) % row_size) for s in range(row_size)])
-    pair = jnp.stack([x, other])
-    parts = [pair]
+    parts = [jnp.stack([x, other])]
     for d in range(1, x_size):
-        perm = [(s, (s // x_size) * x_size + (s % x_size + d) % x_size) for s in range(row_size)]
-        parts.append(lax.ppermute(pair, "row", perm))
+        parts.append(jnp.stack([own[d - 1], lax.ppermute(other, "row", shift(d))]))
     return jnp.concatenate(parts, axis=0)
 
 

time: 51.1 us -> 53.5 us (1.047)
  the two profiles are of different devices: /device:TPU:6 before, /device:TPU:2 now
where the time goes in v2:
time: 53.5 us; the launch traced here: 53.3 us
  starting transfers between devices  30.2 us (56%)
  waiting for transfers between devices  11.9 us (22%)
  Pallas kernels  5.69 us (11%)
  local copies, waits for them, and re-layouts  4.35 us (8%)
  matrix products  0.78 us (1%)
    ppermute x6, starting transfers between devices, reduce_over_rep(): lax.ppermute(lax.dynamic_index_in_dim(part, (y + dy) % 4, 1, keepdims=Fal...  9.82 us
    ppermute x3, starting transfers between devices, reduce_over_rep(): out = out + lax.ppermute(blocks[d], 'rep', z_pairs(rep_size, z_size, d))  9.45 us
    pallas_call x1, Pallas kernels, accumulate_slots(): pl.pallas_call(slot_kernel, grid_spec=grid_spec, out_shape=[half, half],...  5.69 us
    ppermute x3, starting transfers between devices, gather_over_row(): own = [lax.ppermute(x, 'row', shift(d)) for d in range(1, x_size)]  4.76 us
    ppermute x3, waiting for transfers between devices, reduce_over_rep(): out = out + lax.ppermute(blocks[d], 'rep', z_pairs(rep_size, z_size, d))  3.92 us
    ppermute x3, waiting for transfers between devices, gather_over_row(): parts.append(jnp.stack([own[d - 1], lax.ppermute(other, 'row', shift(d))]))  3.83 us
    ppermute x3, starting transfers between devices, gather_over_row(): parts.append(jnp.stack([own[d - 1], lax.ppermute(other, 'row', shift(d))]))  3.58 us
    ppermute x6, waiting for transfers between devices, reduce_over_rep(): lax.ppermute(lax.dynamic_index_in_dim(part, (y + dy) % 4, 1, keepdims=Fal...  2.92 us
  transfers between devices with their start and end apart: 18, of which 7 were waited for; matrix products, arithmetic and copies ran while one was open for 5% of the time, Pallas kernels for 0%

profile of v2, /device:TPU:2, one launch (start us, length us, event | category | flops | bytes accessed | tf_op | source)
XLA Modules:
  0.0 53.3 jit_solution(13138732681658490372)
XLA Ops:
  0.0 0.0 copy-start
  0.0 1.9 %collective-permute-start = (bf16[128,128]{1,0:T(8,128)(2,1)}, bf16[128,128]{1,0:T(8,128)(2,1)S(1)}, u32[]{:S(2)}, u32[]{:S(2)}) collective-permute-start(bf16[128,128]{1,0:T(8,128)(2,1)} %param.7), channel_id=1, source_target_pairs={{0,128},{32,160},{64,192},{96,224},{128,0},{160,32},{192,64},{224,... | collective-permute-start | bytes 98312 | tf_op jit(solution)/shard_map/ppermute | solution.py:85
  1.9 1.5 %collective-permute-start.1 = (bf16[128,128]{1,0:T(8,128)(2,1)}, bf16[128,128]{1,0:T(8,128)(2,1)S(1)}, u32[]{:S(2)}, u32[]{:S(2)}) collective-permute-start(bf16[128,128]{1,0:T(8,128)(2,1)} %param.7), channel_id=1, source_target_pairs={{0,32},{32,64},{64,96},{96,0},{128,160},{160,192},{192,224},{224,1... | collective-permute-start | bytes 98312 | tf_op jit(solution)/shard_map/ppermute | solution.py:84
  3.4 1.1 %collective-permute-start.3 = (bf16[128,128]{1,0:T(8,128)(2,1)}, bf16[128,128]{1,0:T(8,128)(2,1)S(1)}, u32[]{:S(2)}, u32[]{:S(2)}) collective-permute-start(bf16[128,128]{1,0:T(8,128)(2,1)} %param.7), channel_id=1, source_target_pairs={{0,64},{32,96},{64,0},{96,32},{128,192},{160,224},{192,128},{224,1... | collective-permute-start | bytes 98312 | tf_op jit(solution)/shard_map/ppermute | solution.py:84
  4.5 2.2 %collective-permute-start.5 = (bf16[128,128]{1,0:T(8,128)(2,1)}, bf16[128,128]{1,0:T(8,128)(2,1)S(1)}, u32[]{:S(2)}, u32[]{:S(2)}) collective-permute-start(bf16[128,128]{1,0:T(8,128)(2,1)} %param.7), channel_id=1, source_target_pairs={{0,96},{32,0},{64,32},{96,64},{128,224},{160,128},{192,160},{224,1... | collective-permute-start | bytes 98312 | tf_op jit(solution)/shard_map/ppermute | solution.py:84
  6.7 0.8 %bitcast_dynamic-update-slice_fusion.7 = bf16[8,128,128]{2,1,0:T(8,128)(2,1)S(1)} fusion(bf16[128,128]{1,0:T(8,128)(2,1)} %param.7), kind=kLoop, calls=%fused_computation.34 | loop fusion | bytes 65536
  7.5 1.3 %dynamic_slice.53.count_ref = s32[1]{0:T(128)} dynamic-slice(s32[256]{0:T(256)} %param.11, s32[]{:T(128)S(6)} %select_n.93), dynamic_slice_sizes={1} | dynamic-slice | bytes 12 | tf_op jit(solution)/shard_map/dynamic_slice | solution.py:146
  8.7 0.0 collective-permute-done
  8.7 0.0 collective-permute-start.2
  8.7 3.5 %collective-permute-start.4 = (bf16[128,128]{1,0:T(8,128)(2,1)S(1)}, bf16[128,128]{1,0:T(8,128)(2,1)S(1)}, u32[]{:S(2)}, u32[]{:S(2)}) collective-permute-start(bf16[128,128]{1,0:T(8,128)(2,1)S(1)} %collective-permute-done), channel_id=1, source_target_pairs={{0,64},{32,96},{64,0},{96,32},{128,192},{160,224},{192,128},{224,1... | collective-permute-start | bytes 98312 | tf_op jit(solution)/shard_map/ppermute | solution.py:88
  12.2 0.0 collective-permute-done.1
  12.3 0.1 collective-permute-start.6
  12.4 0.3 collective-permute-done.2
  12.7 0.0 collective-permute-done.3
  12.7 1.5 %collective-permute-done.4 = bf16[128,128]{1,0:T(8,128)(2,1)S(1)} collective-permute-done((bf16[128,128]{1,0:T(8,128)(2,1)S(1)}, bf16[128,128]{1,0:T(8,128)(2,1)S(1)}, u32[]{:S(2)}, u32[]{:S(2)}) %collective-permute-start.4) | collective-permute-done | bytes 32800 | tf_op jit(solution)/shard_map/ppermute | solution.py:88
  14.2 0.0 collective-permute-done.5
  14.2 2.1 %collective-permute-done.6 = bf16[128,128]{1,0:T(8,128)(2,1)S(1)} collective-permute-done((bf16[128,128]{1,0:T(8,128)(2,1)S(1)}, bf16[128,128]{1,0:T(8,128)(2,1)S(1)}, u32[]{:S(2)}, u32[]{:S(2)}) %collective-permute-start.6) | collective-permute-done | bytes 32800 | tf_op jit(solution)/shard_map/ppermute | solution.py:88
  16.3 0.0 copy-start.2
  16.3 0.7 %copy-done.2 = bf16[8,128,128]{2,1,0:T(8,128)(2,1)} copy-done((bf16[8,128,128]{2,1,0:T(8,128)(2,1)}, bf16[8,128,128]{2,1,0:T(8,128)(2,1)S(1)}, u32[]{:S(2)}) %copy-start.2) | copy-done | bytes 262168
  16.9 5.7 %shard_map.73 = (f32[16,128,128]{2,1,0:T(8,128)}, f32[16,128,128]{2,1,0:T(8,128)}) custom-call(s32[128]{0:T(128)} %bitcast.64, s32[128]{0:T(128)} %bitcast.65, s32[1]{0:T(128)} %dynamic_slice.53.count_ref, bf16[8,128,128]{2,1,0:T(8,128)(2,1)} %copy-done.2, bf16[128,128,128]{2,1,0:T(8,128)(2,1)} %vals_ref.1), custom_call_target="tpu_custom_call" | custom-call | flops 536870912 | bytes 6553600 | tf_op jit(solution)/shard_map/pallas_call | solution.py:64
  22.6 0.0 copy-start.1
  22.6 1.4 %constant_dynamic-slice_fusion.1 = (f32[1,4,128,128]{3,2,1,0:T(8,128)S(1)}, f32[1,4,128,128]{3,2,1,0:T(8,128)S(1)}, f32[1,4,128,128]{3,2,1,0:T(8,128)S(1)}, f32[1,4,128,128]{3,2,1,0:T(8,128)S(1)}) fusion(f32[4,4,128,128]{3,2,1,0:T(8,128)} %bitcast.63, s32[]{:T(128)S(6)} %select_n.109, s32[]{:T(128)S(6)} %select_n.111, s32[]{:T(128)S(6)} %select_n.98, ...), kind=kLoop, calls=%fused_computation.36 | loop fusion | bytes 2097168 | tf_op jit(solution)/shard_map/jit(dynamic_index_in_dim)/dynamic_slice | solution.py:115
  24.1 0.1 collective-permute-start.11
  24.2 0.6 %collective-permute-start.7 = (f32[2,4,128,128]{3,2,1,0:T(8,128)S(1)}, f32[2,4,128,128]{3,2,1,0:T(8,128)S(1)}, u32[]{:S(2)}, u32[]{:S(2)}) collective-permute-start(f32[2,4,128,128]{3,2,1,0:T(8,128)S(1)} %pad_maximum_fusion), channel_id=1, source_target_pairs={{0,1},{1,0},{2,3},{3,2},{4,5},{5,4},{6,7},{7,6},{8,9},{9,8},{10,11... | collective-permute-start | bytes 1572872 | tf_op jit(solution)/shard_map/ppermute | solution.py:113
  24.8 0.0 copy-done.1
  24.8 0.0 copy-start.3
  24.8 0.1 constant_dynamic-slice_fusion.3
  24.9 1.2 %collective-permute-done.11 = f32[2,4,128,128]{3,2,1,0:T(8,128)S(1)} collective-permute-done((f32[2,4,128,128]{3,2,1,0:T(8,128)S(1)}, f32[2,4,128,128]{3,2,1,0:T(8,128)S(1)}, u32[]{:S(2)}, u32[]{:S(2)}) %collective-permute-start.11) | collective-permute-done | bytes 524320 | tf_op jit(solution)/shard_map/ppermute | solution.py:113
  26.1 0.1 maximum_add_fusion.1
  26.2 1.7 %collective-permute-start.12 = (f32[2,128,128]{2,1,0:T(8,128)S(1)}, f32[2,128,128]{2,1,0:T(8,128)S(1)}, u32[]{:S(2)}, u32[]{:S(2)}) collective-permute-start(f32[2,128,128]{2,1,0:T(8,128)S(1)} %get-tuple-element.17), channel_id=1, source_target_pairs={{0,2},{1,3},{2,4},{3,5},{4,6},{5,7},{6,0},{7,1},{8,10},{9,11},{10,... | collective-permute-start | bytes 393224 | tf_op jit(solution)/shard_map/ppermute | solution.py:125
  27.8 4.0 %collective-permute-start.13 = (f32[2,128,128]{2,1,0:T(8,128)S(1)}, f32[2,128,128]{2,1,0:T(8,128)S(1)}, u32[]{:S(2)}, u32[]{:S(2)}) collective-permute-start(f32[2,128,128]{2,1,0:T(8,128)S(1)} %get-tuple-element.19), channel_id=1, source_target_pairs={{0,4},{1,5},{2,6},{3,7},{4,0},{5,1},{6,2},{7,3},{8,12},{9,13},{10,... | collective-permute-start | bytes 393224 | tf_op jit(solution)/shard_map/ppermute | solution.py:125
  31.8 0.3 collective-permute-start.14
  32.1 0.0 collective-permute-done.7
  32.1 0.1 maximum_add_fusion
  32.2 0.4 collective-permute-start.10
  32.6 1.7 %collective-permute-start.8 = (f32[2,128,128]{2,1,0:T(8,128)S(1)}, f32[2,128,128]{2,1,0:T(8,128)S(1)}, u32[]{:S(2)}, u32[]{:S(2)}) collective-permute-start(f32[2,128,128]{2,1,0:T(8,128)S(1)} %get-tuple-element.20), channel_id=1, source_target_pairs={{0,2},{1,3},{2,4},{3,5},{4,6},{5,7},{6,0},{7,1},{8,10},{9,11},{10,... | collective-permute-start | bytes 393224 | tf_op jit(solution)/shard_map/ppermute | solution.py:125
  34.3 0.0 collective-permute-done.12
  34.3 1.8 %collective-permute-start.9 = (f32[2,128,128]{2,1,0:T(8,128)S(1)}, f32[2,128,128]{2,1,0:T(8,128)S(1)}, u32[]{:S(2)}, u32[]{:S(2)}) collective-permute-start(f32[2,128,128]{2,1,0:T(8,128)S(1)} %get-tuple-element.22), channel_id=1, source_target_pairs={{0,4},{1,5},{2,6},{3,7},{4,0},{5,1},{6,2},{7,3},{8,12},{9,13},{10,... | collective-permute-start | bytes 393224 | tf_op jit(solution)/shard_map/ppermute | solution.py:125
  36.1 2.9 %collective-permute-done.13 = f32[2,128,128]{2,1,0:T(8,128)S(1)} collective-permute-done((f32[2,128,128]{2,1,0:T(8,128)S(1)}, f32[2,128,128]{2,1,0:T(8,128)S(1)}, u32[]{:S(2)}, u32[]{:S(2)}) %collective-permute-start.13) | collective-permute-done | bytes 131104 | tf_op jit(solution)/shard_map/ppermute | solution.py:125
  39.0 0.0 collective-permute-done.14
  39.1 2.2 %collective-permute-start.15 = (f32[128,128]{1,0:T(8,128)S(1)}, f32[128,128]{1,0:T(8,128)S(1)}, u32[]{:S(2)}, u32[]{:S(2)}) collective-permute-start(f32[128,128]{1,0:T(8,128)S(1)} %get-tuple-element.23), channel_id=1, source_target_pairs={{0,8},{1,9},{2,10},{3,11},{4,12},{5,13},{6,14},{7,15},{8,16},{9,17... | collective-permute-start | bytes 196616 | tf_op jit(solution)/shard_map/ppermute | solution.py:138
  41.3 5.2 %collective-permute-start.16 = (f32[128,128]{1,0:T(8,128)S(1)}, f32[128,128]{1,0:T(8,128)S(1)}, u32[]{:S(2)}, u32[]{:S(2)}) collective-permute-start(f32[128,128]{1,0:T(8,128)S(1)} %get-tuple-element.24), channel_id=1, source_target_pairs={{0,16},{1,17},{2,18},{3,19},{4,20},{5,21},{6,22},{7,23},{8,24},{9,... | collective-permute-start | bytes 196616 | tf_op jit(solution)/shard_map/ppermute | solution.py:138
  46.5 0.0 collective-permute-done.10
  46.5 0.0 collective-permute-done.8
  46.5 0.0 collective-permute-done.9
  46.5 2.0 %collective-permute-start.17 = (f32[128,128]{1,0:T(8,128)S(1)}, f32[128,128]{1,0:T(8,128)S(1)}, u32[]{:S(2)}, u32[]{:S(2)}) collective-permute-start(f32[128,128]{1,0:T(8,128)S(1)} %slice_bitcast_fusion), channel_id=1, source_target_pairs={{0,24},{1,25},{2,26},{3,27},{4,28},{5,29},{6,30},{7,31},{8,0},{9,1... | collective-permute-start | bytes 196616 | tf_op jit(solution)/shard_map/ppermute | solution.py:138
  48.6 0.0 collective-permute-done.15
  48.6 2.0 %collective-permute-done.16 = f32[128,128]{1,0:T(8,128)S(1)} collective-permute-done((f32[128,128]{1,0:T(8,128)S(1)}, f32[128,128]{1,0:T(8,128)S(1)}, u32[]{:S(2)}, u32[]{:S(2)}) %collective-permute-start.16) | collective-permute-done | bytes 65568 | tf_op jit(solution)/shard_map/ppermute | solution.py:138
  50.5 2.0 %collective-permute-done.17 = f32[128,128]{1,0:T(8,128)S(1)} collective-permute-done((f32[128,128]{1,0:T(8,128)S(1)}, f32[128,128]{1,0:T(8,128)S(1)}, u32[]{:S(2)}, u32[]{:S(2)}) %collective-permute-start.17) | collective-permute-done | bytes 65568 | tf_op jit(solution)/shard_map/ppermute | solution.py:138
  52.5 0.0 copy-done
  52.5 0.0 copy-done.3
  52.5 0.8 %fusion.1 = bf16[128,256]{1,0:T(8,128)(2,1)} fusion(bf16[128,256]{1,0:T(8,128)(2,1)S(1)} %copy-done, f32[256]{0:T(256)S(1)} %copy-done.3, f32[128,128]{1,0:T(8,128)S(1)} %collective-permute-done.17, f32[128,128]{1,0:T(8,128)S(1)} %collective-permute-done.16, f32[128,128]{1,0:T(8,128)S(1)} %collective-permute-done.15, f32[2,128,128]{2,1,0:T(8,128)S(1)} %fusion.5), kind=kOutput, calls=%fused_computation.2 | convolution fusion | flops 8552448 | bytes 394240 | tf_op jit(solution)/shard_map/dot_general | solution.py:152
  (15 shorter events, 0.3 us)
Async XLA Ops:
  0.0 52.5 %copy-start = (bf16[128,256]{1,0:T(8,128)(2,1)S(1)}, bf16[128,256]{1,0:T(8,128)(2,1)}, u32[]{:S(2)}) copy-start(bf16[128,256]{1,0:T(8,128)(2,1)} %param.12) | copy-start | bytes 196612
  0.0 8.7 %collective-permute-start = (bf16[128,128]{1,0:T(8,128)(2,1)}, bf16[128,128]{1,0:T(8,128)(2,1)S(1)}, u32[]{:S(2)}, u32[]{:S(2)}) collective-permute-start(bf16[128,128]{1,0:T(8,128)(2,1)} %param.7), channel_id=1, source_target_pairs={{0,128},{32,160},{64,192},{96,224},{128,0},{160,32},{192,64},{224,... | collective-permute-start | bytes 98312 | tf_op jit(solution)/shard_map/ppermute | solution.py:85
  1.9 10.3 %collective-permute-start.1 = (bf16[128,128]{1,0:T(8,128)(2,1)}, bf16[128,128]{1,0:T(8,128)(2,1)S(1)}, u32[]{:S(2)}, u32[]{:S(2)}) collective-permute-start(bf16[128,128]{1,0:T(8,128)(2,1)} %param.7), channel_id=1, source_target_pairs={{0,32},{32,64},{64,96},{96,0},{128,160},{160,192},{192,224},{224,1... | collective-permute-start | bytes 98312 | tf_op jit(solution)/shard_map/ppermute | solution.py:84
  3.4 9.3 %collective-permute-start.3 = (bf16[128,128]{1,0:T(8,128)(2,1)}, bf16[128,128]{1,0:T(8,128)(2,1)S(1)}, u32[]{:S(2)}, u32[]{:S(2)}) collective-permute-start(bf16[128,128]{1,0:T(8,128)(2,1)} %param.7), channel_id=1, source_target_pairs={{0,64},{32,96},{64,0},{96,32},{128,192},{160,224},{192,128},{224,1... | collective-permute-start | bytes 98312 | tf_op jit(solution)/shard_map/ppermute | solution.py:84
  4.5 9.6 %collective-permute-start.5 = (bf16[128,128]{1,0:T(8,128)(2,1)}, bf16[128,128]{1,0:T(8,128)(2,1)S(1)}, u32[]{:S(2)}, u32[]{:S(2)}) collective-permute-start(bf16[128,128]{1,0:T(8,128)(2,1)} %param.7), channel_id=1, source_target_pairs={{0,96},{32,0},{64,32},{96,64},{128,224},{160,128},{192,160},{224,1... | collective-permute-start | bytes 98312 | tf_op jit(solution)/shard_map/ppermute | solution.py:84
  8.7 3.9 %collective-permute-start.2 = (bf16[128,128]{1,0:T(8,128)(2,1)S(1)}, bf16[128,128]{1,0:T(8,128)(2,1)S(1)}, u32[]{:S(2)}, u32[]{:S(2)}) collective-permute-start(bf16[128,128]{1,0:T(8,128)(2,1)S(1)} %collective-permute-done), channel_id=1, source_target_pairs={{0,32},{32,64},{64,96},{96,0},{128,160},{160,192},{192,224},{224,1... | collective-permute-start | bytes 98312 | tf_op jit(solution)/shard_map/ppermute | solution.py:88
  8.7 5.4 %collective-permute-start.4 = (bf16[128,128]{1,0:T(8,128)(2,1)S(1)}, bf16[128,128]{1,0:T(8,128)(2,1)S(1)}, u32[]{:S(2)}, u32[]{:S(2)}) collective-permute-start(bf16[128,128]{1,0:T(8,128)(2,1)S(1)} %collective-permute-done), channel_id=1, source_target_pairs={{0,64},{32,96},{64,0},{96,32},{128,192},{160,224},{192,128},{224,1... | collective-permute-start | bytes 98312 | tf_op jit(solution)/shard_map/ppermute | solution.py:88
  12.3 4.0 %collective-permute-start.6 = (bf16[128,128]{1,0:T(8,128)(2,1)S(1)}, bf16[128,128]{1,0:T(8,128)(2,1)S(1)}, u32[]{:S(2)}, u32[]{:S(2)}) collective-permute-start(bf16[128,128]{1,0:T(8,128)(2,1)S(1)} %collective-permute-done), channel_id=1, source_target_pairs={{0,96},{32,0},{64,32},{96,64},{128,224},{160,128},{192,160},{224,1... | collective-permute-start | bytes 98312 | tf_op jit(solution)/shard_map/ppermute | solution.py:88
  16.3 0.7 %copy-start.2 = (bf16[8,128,128]{2,1,0:T(8,128)(2,1)}, bf16[8,128,128]{2,1,0:T(8,128)(2,1)S(1)}, u32[]{:S(2)}) copy-start(bf16[8,128,128]{2,1,0:T(8,128)(2,1)S(1)} %bitcast_dynamic-update-slice_fusion.feats_ref) | copy-start | bytes 786436
  22.6 2.1 %copy-start.1 = (f32[16,128,128]{2,1,0:T(8,128)S(1)}, f32[16,128,128]{2,1,0:T(8,128)}, u32[]{:S(2)}) copy-start(f32[16,128,128]{2,1,0:T(8,128)} %get-tuple-element.7) | copy-start | bytes 3145732
  24.1 2.0 %collective-permute-start.11 = (f32[2,4,128,128]{3,2,1,0:T(8,128)S(1)}, f32[2,4,128,128]{3,2,1,0:T(8,128)S(1)}, u32[]{:S(2)}, u32[]{:S(2)}) collective-permute-start(f32[2,4,128,128]{3,2,1,0:T(8,128)S(1)} %pad_maximum_fusion.1), channel_id=1, source_target_pairs={{0,1},{1,0},{2,3},{3,2},{4,5},{5,4},{6,7},{7,6},{8,9},{9,8},{10,11... | collective-permute-start | bytes 1572872 | tf_op jit(solution)/shard_map/ppermute | solution.py:113
  24.2 7.9 %collective-permute-start.7 = (f32[2,4,128,128]{3,2,1,0:T(8,128)S(1)}, f32[2,4,128,128]{3,2,1,0:T(8,128)S(1)}, u32[]{:S(2)}, u32[]{:S(2)}) collective-permute-start(f32[2,4,128,128]{3,2,1,0:T(8,128)S(1)} %pad_maximum_fusion), channel_id=1, source_target_pairs={{0,1},{1,0},{2,3},{3,2},{4,5},{5,4},{6,7},{7,6},{8,9},{9,8},{10,11... | collective-permute-start | bytes 1572872 | tf_op jit(solution)/shard_map/ppermute | solution.py:113
  24.8 27.7 %copy-start.3 = (f32[256]{0:T(256)S(1)}, f32[256]{0:T(256)}, u32[]{:S(2)}) copy-start(f32[256]{0:T(256)} %param.13) | copy-start | bytes 3076
  26.2 8.1 %collective-permute-start.12 = (f32[2,128,128]{2,1,0:T(8,128)S(1)}, f32[2,128,128]{2,1,0:T(8,128)S(1)}, u32[]{:S(2)}, u32[]{:S(2)}) collective-permute-start(f32[2,128,128]{2,1,0:T(8,128)S(1)} %get-tuple-element.17), channel_id=1, source_target_pairs={{0,2},{1,3},{2,4},{3,5},{4,6},{5,7},{6,0},{7,1},{8,10},{9,11},{10,... | collective-permute-start | bytes 393224 | tf_op jit(solution)/shard_map/ppermute | solution.py:125
  27.8 11.2 %collective-permute-start.13 = (f32[2,128,128]{2,1,0:T(8,128)S(1)}, f32[2,128,128]{2,1,0:T(8,128)S(1)}, u32[]{:S(2)}, u32[]{:S(2)}) collective-permute-start(f32[2,128,128]{2,1,0:T(8,128)S(1)} %get-tuple-element.19), channel_id=1, source_target_pairs={{0,4},{1,5},{2,6},{3,7},{4,0},{5,1},{6,2},{7,3},{8,12},{9,13},{10,... | collective-permute-start | bytes 393224 | tf_op jit(solution)/shard_map/ppermute | solution.py:125
  31.8 7.2 %collective-permute-start.14 = (f32[2,128,128]{2,1,0:T(8,128)S(1)}, f32[2,128,128]{2,1,0:T(8,128)S(1)}, u32[]{:S(2)}, u32[]{:S(2)}) collective-permute-start(f32[2,128,128]{2,1,0:T(8,128)S(1)} %get-tuple-element.18), channel_id=1, source_target_pairs={{0,6},{1,7},{2,0},{3,1},{4,2},{5,3},{6,4},{7,5},{8,14},{9,15},{10,... | collective-permute-start | bytes 393224 | tf_op jit(solution)/shard_map/ppermute | solution.py:125
  32.2 14.3 %collective-permute-start.10 = (f32[2,128,128]{2,1,0:T(8,128)S(1)}, f32[2,128,128]{2,1,0:T(8,128)S(1)}, u32[]{:S(2)}, u32[]{:S(2)}) collective-permute-start(f32[2,128,128]{2,1,0:T(8,128)S(1)} %get-tuple-element.21), channel_id=1, source_target_pairs={{0,6},{1,7},{2,0},{3,1},{4,2},{5,3},{6,4},{7,5},{8,14},{9,15},{10,... | collective-permute-start | bytes 393224 | tf_op jit(solution)/shard_map/ppermute | solution.py:125
  32.6 13.9 %collective-permute-start.8 = (f32[2,128,128]{2,1,0:T(8,128)S(1)}, f32[2,128,128]{2,1,0:T(8,128)S(1)}, u32[]{:S(2)}, u32[]{:S(2)}) collective-permute-start(f32[2,128,128]{2,1,0:T(8,128)S(1)} %get-tuple-element.20), channel_id=1, source_target_pairs={{0,2},{1,3},{2,4},{3,5},{4,6},{5,7},{6,0},{7,1},{8,10},{9,11},{10,... | collective-permute-start | bytes 393224 | tf_op jit(solution)/shard_map/ppermute | solution.py:125
  34.3 12.2 %collective-permute-start.9 = (f32[2,128,128]{2,1,0:T(8,128)S(1)}, f32[2,128,128]{2,1,0:T(8,128)S(1)}, u32[]{:S(2)}, u32[]{:S(2)}) collective-permute-start(f32[2,128,128]{2,1,0:T(8,128)S(1)} %get-tuple-element.22), channel_id=1, source_target_pairs={{0,4},{1,5},{2,6},{3,7},{4,0},{5,1},{6,2},{7,3},{8,12},{9,13},{10,... | collective-permute-start | bytes 393224 | tf_op jit(solution)/shard_map/ppermute | solution.py:125
  39.1 9.5 %collective-permute-start.15 = (f32[128,128]{1,0:T(8,128)S(1)}, f32[128,128]{1,0:T(8,128)S(1)}, u32[]{:S(2)}, u32[]{:S(2)}) collective-permute-start(f32[128,128]{1,0:T(8,128)S(1)} %get-tuple-element.23), channel_id=1, source_target_pairs={{0,8},{1,9},{2,10},{3,11},{4,12},{5,13},{6,14},{7,15},{8,16},{9,17... | collective-permute-start | bytes 196616 | tf_op jit(solution)/shard_map/ppermute | solution.py:138
  41.3 9.3 %collective-permute-start.16 = (f32[128,128]{1,0:T(8,128)S(1)}, f32[128,128]{1,0:T(8,128)S(1)}, u32[]{:S(2)}, u32[]{:S(2)}) collective-permute-start(f32[128,128]{1,0:T(8,128)S(1)} %get-tuple-element.24), channel_id=1, source_target_pairs={{0,16},{1,17},{2,18},{3,19},{4,20},{5,21},{6,22},{7,23},{8,24},{9,... | collective-permute-start | bytes 196616 | tf_op jit(solution)/shard_map/ppermute | solution.py:138
  46.5 6.0 %collective-permute-start.17 = (f32[128,128]{1,0:T(8,128)S(1)}, f32[128,128]{1,0:T(8,128)S(1)}, u32[]{:S(2)}, u32[]{:S(2)}) collective-permute-start(f32[128,128]{1,0:T(8,128)S(1)} %slice_bitcast_fusion), channel_id=1, source_target_pairs={{0,24},{1,25},{2,26},{3,27},{4,28},{5,29},{6,30},{7,31},{8,0},{9,1... | collective-permute-start | bytes 196616 | tf_op jit(solution)/shard_map/ppermute | solution.py:138

commit v3 on v2

--- a/solution.py
+++ b/solution.py
@@ -9,7 +9,7 @@
 GROUP = 64
 
 
-def slot_kernel(rows_ref, cols_ref, count_ref, feats_ref, vals_ref, keep_ref, send_ref, acc_ref):
+def slot_kernel(rows_ref, cols_ref, count_ref, feats_ref, vals_ref, keep_ref, send_ref, acc_ref, sems):
     g = pl.program_id(0)
     live = count_ref[0]
     row_index = lax.axis_index("row")
@@ -35,9 +35,14 @@
 
     @pl.when(g == pl.num_programs(0) - 1)
     def _():
+        copies = []
         for t in range(keep_ref.shape[0]):
-            keep_ref[t] = acc_ref[2 * t + core]
-            send_ref[t] = acc_ref[2 * t + 1 - core]
+            for n, (dst, src) in enumerate(((keep_ref, 2 * t + core), (send_ref, 2 * t + 1 - core))):
+                cp = pltpu.make_async_copy(acc_ref.at[src], dst.at[t], sems.at[2 * t + n])
+                cp.start()
+                copies.append(cp)
+        for cp in copies:
+            cp.wait()
 
 
 def accumulate_slots(rows, cols, count, feats, vals, rep_size):
@@ -58,8 +63,11 @@
             pl.BlockSpec((sections, blk, width), lambda g, *_: (0, 0, 0)),
             pl.BlockSpec((GROUP, blk, blk), vals_map),
         ],
-        out_specs=[half_spec, half_spec],
-        scratch_shapes=[pltpu.VMEM((rep_size, blk, width), jnp.float32)],
+        out_specs=[pl.BlockSpec(memory_space=pl.ANY)] * 2,
+        scratch_shapes=[
+            pltpu.VMEM((rep_size, blk, width), jnp.float32),
+            pltpu.SemaphoreType.DMA((rep_size,)),
+        ],
     )
     return pl.pallas_call(
         slot_kernel,
@@ -117,16 +125,10 @@
             "rep",
             [(i, i ^ 1) for i in range(rep_size)],
         )
-        part = jnp.stack(
-            [lax.dynamic_index_in_dim(keep, (z + d) % z_size, 0, keepdims=False) for d in shifts]
-        ) + got
+        part = jnp.stack([lax.dynamic_index_in_dim(keep, (z + d) % z_size, 0, keepdims=False) for d in shifts]) + got
         acc = lax.dynamic_index_in_dim(part, y, 1, keepdims=False)
         got = [
-            lax.ppermute(
-                lax.dynamic_index_in_dim(part, (y + dy) % 4, 1, keepdims=False),
-                "rep",
-                y_pairs(rep_size, dy),
-            )
+            lax.ppermute(lax.dynamic_index_in_dim(part, (y + dy) % 4, 1, keepdims=False), "rep", y_pairs(rep_size, dy))
             for dy in (1, 2, 3)
         ]
         for piece in got:

time: 53.5 us -> 53.7 us (level)
  no operation moved by 1% of the time
where the time goes in v3:
time: 53.7 us; the launch traced here: 53.4 us
  starting transfers between devices  30.2 us (56%)
  waiting for transfers between devices  11.9 us (22%)
  Pallas kernels  5.82 us (11%)
  local copies, waits for them, and re-layouts  4.36 us (8%)
  matrix products  0.78 us (1%)
    ppermute x6, starting transfers between devices, reduce_over_rep(): lax.ppermute(lax.dynamic_index_in_dim(part, (y + dy) % 4, 1, keepdims=Fal...  9.81 us
    ppermute x3, starting transfers between devices, reduce_over_rep(): out = out + lax.ppermute(blocks[d], 'rep', z_pairs(rep_size, z_size, d))  9.45 us
    pallas_call x1, Pallas kernels, accumulate_slots(): pl.pallas_call(slot_kernel, grid_spec=grid_spec, out_shape=[half, half],...  5.82 us
    ppermute x3, starting transfers between devices, gather_over_row(): own = [lax.ppermute(x, 'row', shift(d)) for d in range(1, x_size)]  4.76 us
    ppermute x3, waiting for transfers between devices, reduce_over_rep(): out = out + lax.ppermute(blocks[d], 'rep', z_pairs(rep_size, z_size, d))  3.92 us
    ppermute x3, waiting for transfers between devices, gather_over_row(): parts.append(jnp.stack([own[d - 1], lax.ppermute(other, 'row', shift(d))]))  3.83 us
    ppermute x3, starting transfers between devices, gather_over_row(): parts.append(jnp.stack([own[d - 1], lax.ppermute(other, 'row', shift(d))]))  3.58 us
    ppermute x6, waiting for transfers between devices, reduce_over_rep(): lax.ppermute(lax.dynamic_index_in_dim(part, (y + dy) % 4, 1, keepdims=Fal...  2.92 us
  transfers between devices with their start and end apart: 18, of which 7 were waited for; matrix products, arithmetic and copies ran while one was open for 5% of the time, Pallas kernels for 0%

profile of v3, /device:TPU:2, one launch (start us, length us, event | category | flops | bytes accessed | tf_op | source)
XLA Modules:
  0.0 53.4 jit_solution(1578837669912351650)
XLA Ops:
  0.0 0.0 copy-start
  0.0 1.9 %collective-permute-start = (bf16[128,128]{1,0:T(8,128)(2,1)}, bf16[128,128]{1,0:T(8,128)(2,1)S(1)}, u32[]{:S(2)}, u32[]{:S(2)}) collective-permute-start(bf16[128,128]{1,0:T(8,128)(2,1)} %param.7), channel_id=1, source_target_pairs={{0,128},{32,160},{64,192},{96,224},{128,0},{160,32},{192,64},{224,... | collective-permute-start | bytes 98312 | tf_op jit(solution)/shard_map/ppermute | solution.py:93
  1.9 1.5 %collective-permute-start.1 = (bf16[128,128]{1,0:T(8,128)(2,1)}, bf16[128,128]{1,0:T(8,128)(2,1)S(1)}, u32[]{:S(2)}, u32[]{:S(2)}) collective-permute-start(bf16[128,128]{1,0:T(8,128)(2,1)} %param.7), channel_id=1, source_target_pairs={{0,32},{32,64},{64,96},{96,0},{128,160},{160,192},{192,224},{224,1... | collective-permute-start | bytes 98312 | tf_op jit(solution)/shard_map/ppermute | solution.py:92
  3.4 1.1 %collective-permute-start.3 = (bf16[128,128]{1,0:T(8,128)(2,1)}, bf16[128,128]{1,0:T(8,128)(2,1)S(1)}, u32[]{:S(2)}, u32[]{:S(2)}) collective-permute-start(bf16[128,128]{1,0:T(8,128)(2,1)} %param.7), channel_id=1, source_target_pairs={{0,64},{32,96},{64,0},{96,32},{128,192},{160,224},{192,128},{224,1... | collective-permute-start | bytes 98312 | tf_op jit(solution)/shard_map/ppermute | solution.py:92
  4.5 2.2 %collective-permute-start.5 = (bf16[128,128]{1,0:T(8,128)(2,1)}, bf16[128,128]{1,0:T(8,128)(2,1)S(1)}, u32[]{:S(2)}, u32[]{:S(2)}) collective-permute-start(bf16[128,128]{1,0:T(8,128)(2,1)} %param.7), channel_id=1, source_target_pairs={{0,96},{32,0},{64,32},{96,64},{128,224},{160,128},{192,160},{224,1... | collective-permute-start | bytes 98312 | tf_op jit(solution)/shard_map/ppermute | solution.py:92
  6.7 0.8 %bitcast_dynamic-update-slice_fusion.7 = bf16[8,128,128]{2,1,0:T(8,128)(2,1)S(1)} fusion(bf16[128,128]{1,0:T(8,128)(2,1)} %param.7), kind=kLoop, calls=%fused_computation.34 | loop fusion | bytes 65536
  7.5 1.3 %dynamic_slice.53.count_ref = s32[1]{0:T(128)} dynamic-slice(s32[256]{0:T(256)} %param.11, s32[]{:T(128)S(6)} %select_n.93), dynamic_slice_sizes={1} | dynamic-slice | bytes 12 | tf_op jit(solution)/shard_map/dynamic_slice | solution.py:148
  8.7 0.0 collective-permute-done
  8.7 0.0 collective-permute-start.2
  8.7 3.5 %collective-permute-start.4 = (bf16[128,128]{1,0:T(8,128)(2,1)S(1)}, bf16[128,128]{1,0:T(8,128)(2,1)S(1)}, u32[]{:S(2)}, u32[]{:S(2)}) collective-permute-start(bf16[128,128]{1,0:T(8,128)(2,1)S(1)} %collective-permute-done), channel_id=1, source_target_pairs={{0,64},{32,96},{64,0},{96,32},{128,192},{160,224},{192,128},{224,1... | collective-permute-start | bytes 98312 | tf_op jit(solution)/shard_map/ppermute | solution.py:96
  12.2 0.0 collective-permute-done.1
  12.3 0.1 collective-permute-start.6
  12.4 0.3 collective-permute-done.2
  12.7 0.0 collective-permute-done.3
  12.7 1.5 %collective-permute-done.4 = bf16[128,128]{1,0:T(8,128)(2,1)S(1)} collective-permute-done((bf16[128,128]{1,0:T(8,128)(2,1)S(1)}, bf16[128,128]{1,0:T(8,128)(2,1)S(1)}, u32[]{:S(2)}, u32[]{:S(2)}) %collective-permute-start.4) | collective-permute-done | bytes 32800 | tf_op jit(solution)/shard_map/ppermute | solution.py:96
  14.2 0.0 collective-permute-done.5
  14.2 2.1 %collective-permute-done.6 = bf16[128,128]{1,0:T(8,128)(2,1)S(1)} collective-permute-done((bf16[128,128]{1,0:T(8,128)(2,1)S(1)}, bf16[128,128]{1,0:T(8,128)(2,1)S(1)}, u32[]{:S(2)}, u32[]{:S(2)}) %collective-permute-start.6) | collective-permute-done | bytes 32800 | tf_op jit(solution)/shard_map/ppermute | solution.py:96
  16.3 0.0 copy-start.2
  16.3 0.7 %copy-done.2 = bf16[8,128,128]{2,1,0:T(8,128)(2,1)} copy-done((bf16[8,128,128]{2,1,0:T(8,128)(2,1)}, bf16[8,128,128]{2,1,0:T(8,128)(2,1)S(1)}, u32[]{:S(2)}) %copy-start.2) | copy-done | bytes 262168
  16.9 5.8 %shard_map.73 = (f32[16,128,128]{2,1,0:T(8,128)}, f32[16,128,128]{2,1,0:T(8,128)}) custom-call(s32[128]{0:T(128)} %bitcast.64, s32[128]{0:T(128)} %bitcast.65, s32[1]{0:T(128)} %dynamic_slice.53.count_ref, bf16[8,128,128]{2,1,0:T(8,128)(2,1)} %copy-done.2, bf16[128,128,128]{2,1,0:T(8,128)(2,1)} %vals_ref.1), custom_call_target="tpu_custom_call" | custom-call | flops 536870912 | bytes 6553600 | tf_op jit(solution)/shard_map/pallas_call | solution.py:72
  22.8 0.0 copy-start.1
  22.8 1.4 %constant_dynamic-slice_fusion.1 = (f32[1,4,128,128]{3,2,1,0:T(8,128)S(1)}, f32[1,4,128,128]{3,2,1,0:T(8,128)S(1)}, f32[1,4,128,128]{3,2,1,0:T(8,128)S(1)}, f32[1,4,128,128]{3,2,1,0:T(8,128)S(1)}) fusion(f32[4,4,128,128]{3,2,1,0:T(8,128)} %bitcast.63, s32[]{:T(128)S(6)} %select_n.109, s32[]{:T(128)S(6)} %select_n.111, s32[]{:T(128)S(6)} %select_n.98, ...), kind=kLoop, calls=%fused_computation.36 | loop fusion | bytes 2097168 | tf_op jit(solution)/shard_map/jit(dynamic_index_in_dim)/dynamic_slice | solution.py:123
  24.2 0.1 collective-permute-start.11
  24.4 0.6 %collective-permute-start.7 = (f32[2,4,128,128]{3,2,1,0:T(8,128)S(1)}, f32[2,4,128,128]{3,2,1,0:T(8,128)S(1)}, u32[]{:S(2)}, u32[]{:S(2)}) collective-permute-start(f32[2,4,128,128]{3,2,1,0:T(8,128)S(1)} %pad_maximum_fusion), channel_id=1, source_target_pairs={{0,1},{1,0},{2,3},{3,2},{4,5},{5,4},{6,7},{7,6},{8,9},{9,8},{10,11... | collective-permute-start | bytes 1572872 | tf_op jit(solution)/shard_map/ppermute | solution.py:121
  24.9 0.0 copy-done.1
  24.9 0.0 copy-start.3
  24.9 0.1 constant_dynamic-slice_fusion.3
  25.0 1.2 %collective-permute-done.11 = f32[2,4,128,128]{3,2,1,0:T(8,128)S(1)} collective-permute-done((f32[2,4,128,128]{3,2,1,0:T(8,128)S(1)}, f32[2,4,128,128]{3,2,1,0:T(8,128)S(1)}, u32[]{:S(2)}, u32[]{:S(2)}) %collective-permute-start.11) | collective-permute-done | bytes 524320 | tf_op jit(solution)/shard_map/ppermute | solution.py:121
  26.2 0.1 maximum_add_fusion.1
  26.3 1.7 %collective-permute-start.12 = (f32[2,128,128]{2,1,0:T(8,128)S(1)}, f32[2,128,128]{2,1,0:T(8,128)S(1)}, u32[]{:S(2)}, u32[]{:S(2)}) collective-permute-start(f32[2,128,128]{2,1,0:T(8,128)S(1)} %get-tuple-element.17), channel_id=1, source_target_pairs={{0,2},{1,3},{2,4},{3,5},{4,6},{5,7},{6,0},{7,1},{8,10},{9,11},{10,... | collective-permute-start | bytes 393224 | tf_op jit(solution)/shard_map/ppermute | solution.py:131
  28.0 4.0 %collective-permute-start.13 = (f32[2,128,128]{2,1,0:T(8,128)S(1)}, f32[2,128,128]{2,1,0:T(8,128)S(1)}, u32[]{:S(2)}, u32[]{:S(2)}) collective-permute-start(f32[2,128,128]{2,1,0:T(8,128)S(1)} %get-tuple-element.19), channel_id=1, source_target_pairs={{0,4},{1,5},{2,6},{3,7},{4,0},{5,1},{6,2},{7,3},{8,12},{9,13},{10,... | collective-permute-start | bytes 393224 | tf_op jit(solution)/shard_map/ppermute | solution.py:131
  32.0 0.3 collective-permute-start.14
  32.2 0.0 collective-permute-done.7
  32.2 0.1 maximum_add_fusion
  32.3 0.4 collective-permute-start.10
  32.7 1.7 %collective-permute-start.8 = (f32[2,128,128]{2,1,0:T(8,128)S(1)}, f32[2,128,128]{2,1,0:T(8,128)S(1)}, u32[]{:S(2)}, u32[]{:S(2)}) collective-permute-start(f32[2,128,128]{2,1,0:T(8,128)S(1)} %get-tuple-element.20), channel_id=1, source_target_pairs={{0,2},{1,3},{2,4},{3,5},{4,6},{5,7},{6,0},{7,1},{8,10},{9,11},{10,... | collective-permute-start | bytes 393224 | tf_op jit(solution)/shard_map/ppermute | solution.py:131
  34.4 0.0 collective-permute-done.12
  34.4 1.8 %collective-permute-start.9 = (f32[2,128,128]{2,1,0:T(8,128)S(1)}, f32[2,128,128]{2,1,0:T(8,128)S(1)}, u32[]{:S(2)}, u32[]{:S(2)}) collective-permute-start(f32[2,128,128]{2,1,0:T(8,128)S(1)} %get-tuple-element.22), channel_id=1, source_target_pairs={{0,4},{1,5},{2,6},{3,7},{4,0},{5,1},{6,2},{7,3},{8,12},{9,13},{10,... | collective-permute-start | bytes 393224 | tf_op jit(solution)/shard_map/ppermute | solution.py:131
  36.2 2.9 %collective-permute-done.13 = f32[2,128,128]{2,1,0:T(8,128)S(1)} collective-permute-done((f32[2,128,128]{2,1,0:T(8,128)S(1)}, f32[2,128,128]{2,1,0:T(8,128)S(1)}, u32[]{:S(2)}, u32[]{:S(2)}) %collective-permute-start.13) | collective-permute-done | bytes 131104 | tf_op jit(solution)/shard_map/ppermute | solution.py:131
  39.1 0.0 collective-permute-done.14
  39.2 2.2 %collective-permute-start.15 = (f32[128,128]{1,0:T(8,128)S(1)}, f32[128,128]{1,0:T(8,128)S(1)}, u32[]{:S(2)}, u32[]{:S(2)}) collective-permute-start(f32[128,128]{1,0:T(8,128)S(1)} %get-tuple-element.23), channel_id=1, source_target_pairs={{0,8},{1,9},{2,10},{3,11},{4,12},{5,13},{6,14},{7,15},{8,16},{9,17... | collective-permute-start | bytes 196616 | tf_op jit(solution)/shard_map/ppermute | solution.py:140
  41.4 5.2 %collective-permute-start.16 = (f32[128,128]{1,0:T(8,128)S(1)}, f32[128,128]{1,0:T(8,128)S(1)}, u32[]{:S(2)}, u32[]{:S(2)}) collective-permute-start(f32[128,128]{1,0:T(8,128)S(1)} %get-tuple-element.24), channel_id=1, source_target_pairs={{0,16},{1,17},{2,18},{3,19},{4,20},{5,21},{6,22},{7,23},{8,24},{9,... | collective-permute-start | bytes 196616 | tf_op jit(solution)/shard_map/ppermute | solution.py:140
  46.6 0.0 collective-permute-done.10
  46.6 0.0 collective-permute-done.8
  46.6 0.0 collective-permute-done.9
  46.7 2.0 %collective-permute-start.17 = (f32[128,128]{1,0:T(8,128)S(1)}, f32[128,128]{1,0:T(8,128)S(1)}, u32[]{:S(2)}, u32[]{:S(2)}) collective-permute-start(f32[128,128]{1,0:T(8,128)S(1)} %slice_bitcast_fusion), channel_id=1, source_target_pairs={{0,24},{1,25},{2,26},{3,27},{4,28},{5,29},{6,30},{7,31},{8,0},{9,1... | collective-permute-start | bytes 196616 | tf_op jit(solution)/shard_map/ppermute | solution.py:140
  48.7 0.0 collective-permute-done.15
  48.7 2.0 %collective-permute-done.16 = f32[128,128]{1,0:T(8,128)S(1)} collective-permute-done((f32[128,128]{1,0:T(8,128)S(1)}, f32[128,128]{1,0:T(8,128)S(1)}, u32[]{:S(2)}, u32[]{:S(2)}) %collective-permute-start.16) | collective-permute-done | bytes 65568 | tf_op jit(solution)/shard_map/ppermute | solution.py:140
  50.7 2.0 %collective-permute-done.17 = f32[128,128]{1,0:T(8,128)S(1)} collective-permute-done((f32[128,128]{1,0:T(8,128)S(1)}, f32[128,128]{1,0:T(8,128)S(1)}, u32[]{:S(2)}, u32[]{:S(2)}) %collective-permute-start.17) | collective-permute-done | bytes 65568 | tf_op jit(solution)/shard_map/ppermute | solution.py:140
  52.6 0.0 copy-done
  52.6 0.0 copy-done.3
  52.6 0.8 %fusion.1 = bf16[128,256]{1,0:T(8,128)(2,1)} fusion(bf16[128,256]{1,0:T(8,128)(2,1)S(1)} %copy-done, f32[256]{0:T(256)S(1)} %copy-done.3, f32[128,128]{1,0:T(8,128)S(1)} %collective-permute-done.17, f32[128,128]{1,0:T(8,128)S(1)} %collective-permute-done.16, f32[128,128]{1,0:T(8,128)S(1)} %collective-permute-done.15, f32[2,128,128]{2,1,0:T(8,128)S(1)} %fusion.5), kind=kOutput, calls=%fused_computation.2 | convolution fusion | flops 8552448 | bytes 394240 | tf_op jit(solution)/shard_map/dot_general | solution.py:154
  (15 shorter events, 0.3 us)
Async XLA Ops:
  0.0 52.6 %copy-start = (bf16[128,256]{1,0:T(8,128)(2,1)S(1)}, bf16[128,256]{1,0:T(8,128)(2,1)}, u32[]{:S(2)}) copy-start(bf16[128,256]{1,0:T(8,128)(2,1)} %param.12) | copy-start | bytes 196612
  0.0 8.7 %collective-permute-start = (bf16[128,128]{1,0:T(8,128)(2,1)}, bf16[128,128]{1,0:T(8,128)(2,1)S(1)}, u32[]{:S(2)}, u32[]{:S(2)}) collective-permute-start(bf16[128,128]{1,0:T(8,128)(2,1)} %param.7), channel_id=1, source_target_pairs={{0,128},{32,160},{64,192},{96,224},{128,0},{160,32},{192,64},{224,... | collective-permute-start | bytes 98312 | tf_op jit(solution)/shard_map/ppermute | solution.py:93
  1.9 10.3 %collective-permute-start.1 = (bf16[128,128]{1,0:T(8,128)(2,1)}, bf16[128,128]{1,0:T(8,128)(2,1)S(1)}, u32[]{:S(2)}, u32[]{:S(2)}) collective-permute-start(bf16[128,128]{1,0:T(8,128)(2,1)} %param.7), channel_id=1, source_target_pairs={{0,32},{32,64},{64,96},{96,0},{128,160},{160,192},{192,224},{224,1... | collective-permute-start | bytes 98312 | tf_op jit(solution)/shard_map/ppermute | solution.py:92
  3.4 9.3 %collective-permute-start.3 = (bf16[128,128]{1,0:T(8,128)(2,1)}, bf16[128,128]{1,0:T(8,128)(2,1)S(1)}, u32[]{:S(2)}, u32[]{:S(2)}) collective-permute-start(bf16[128,128]{1,0:T(8,128)(2,1)} %param.7), channel_id=1, source_target_pairs={{0,64},{32,96},{64,0},{96,32},{128,192},{160,224},{192,128},{224,1... | collective-permute-start | bytes 98312 | tf_op jit(solution)/shard_map/ppermute | solution.py:92
  4.5 9.6 %collective-permute-start.5 = (bf16[128,128]{1,0:T(8,128)(2,1)}, bf16[128,128]{1,0:T(8,128)(2,1)S(1)}, u32[]{:S(2)}, u32[]{:S(2)}) collective-permute-start(bf16[128,128]{1,0:T(8,128)(2,1)} %param.7), channel_id=1, source_target_pairs={{0,96},{32,0},{64,32},{96,64},{128,224},{160,128},{192,160},{224,1... | collective-permute-start | bytes 98312 | tf_op jit(solution)/shard_map/ppermute | solution.py:92
  8.7 3.9 %collective-permute-start.2 = (bf16[128,128]{1,0:T(8,128)(2,1)S(1)}, bf16[128,128]{1,0:T(8,128)(2,1)S(1)}, u32[]{:S(2)}, u32[]{:S(2)}) collective-permute-start(bf16[128,128]{1,0:T(8,128)(2,1)S(1)} %collective-permute-done), channel_id=1, source_target_pairs={{0,32},{32,64},{64,96},{96,0},{128,160},{160,192},{192,224},{224,1... | collective-permute-start | bytes 98312 | tf_op jit(solution)/shard_map/ppermute | solution.py:96
  8.7 5.4 %collective-permute-start.4 = (bf16[128,128]{1,0:T(8,128)(2,1)S(1)}, bf16[128,128]{1,0:T(8,128)(2,1)S(1)}, u32[]{:S(2)}, u32[]{:S(2)}) collective-permute-start(bf16[128,128]{1,0:T(8,128)(2,1)S(1)} %collective-permute-done), channel_id=1, source_target_pairs={{0,64},{32,96},{64,0},{96,32},{128,192},{160,224},{192,128},{224,1... | collective-permute-start | bytes 98312 | tf_op jit(solution)/shard_map/ppermute | solution.py:96
  12.3 4.0 %collective-permute-start.6 = (bf16[128,128]{1,0:T(8,128)(2,1)S(1)}, bf16[128,128]{1,0:T(8,128)(2,1)S(1)}, u32[]{:S(2)}, u32[]{:S(2)}) collective-permute-start(bf16[128,128]{1,0:T(8,128)(2,1)S(1)} %collective-permute-done), channel_id=1, source_target_pairs={{0,96},{32,0},{64,32},{96,64},{128,224},{160,128},{192,160},{224,1... | collective-permute-start | bytes 98312 | tf_op jit(solution)/shard_map/ppermute | solution.py:96
  16.3 0.7 %copy-start.2 = (bf16[8,128,128]{2,1,0:T(8,128)(2,1)}, bf16[8,128,128]{2,1,0:T(8,128)(2,1)S(1)}, u32[]{:S(2)}) copy-start(bf16[8,128,128]{2,1,0:T(8,128)(2,1)S(1)} %bitcast_dynamic-update-slice_fusion.feats_ref) | copy-start | bytes 786436
  22.8 2.2 %copy-start.1 = (f32[16,128,128]{2,1,0:T(8,128)S(1)}, f32[16,128,128]{2,1,0:T(8,128)}, u32[]{:S(2)}) copy-start(f32[16,128,128]{2,1,0:T(8,128)} %get-tuple-element.7) | copy-start | bytes 3145732
  24.2 2.0 %collective-permute-start.11 = (f32[2,4,128,128]{3,2,1,0:T(8,128)S(1)}, f32[2,4,128,128]{3,2,1,0:T(8,128)S(1)}, u32[]{:S(2)}, u32[]{:S(2)}) collective-permute-start(f32[2,4,128,128]{3,2,1,0:T(8,128)S(1)} %pad_maximum_fusion.1), channel_id=1, source_target_pairs={{0,1},{1,0},{2,3},{3,2},{4,5},{5,4},{6,7},{7,6},{8,9},{9,8},{10,11... | collective-permute-start | bytes 1572872 | tf_op jit(solution)/shard_map/ppermute | solution.py:121
  24.4 7.9 %collective-permute-start.7 = (f32[2,4,128,128]{3,2,1,0:T(8,128)S(1)}, f32[2,4,128,128]{3,2,1,0:T(8,128)S(1)}, u32[]{:S(2)}, u32[]{:S(2)}) collective-permute-start(f32[2,4,128,128]{3,2,1,0:T(8,128)S(1)} %pad_maximum_fusion), channel_id=1, source_target_pairs={{0,1},{1,0},{2,3},{3,2},{4,5},{5,4},{6,7},{7,6},{8,9},{9,8},{10,11... | collective-permute-start | bytes 1572872 | tf_op jit(solution)/shard_map/ppermute | solution.py:121
  24.9 27.7 %copy-start.3 = (f32[256]{0:T(256)S(1)}, f32[256]{0:T(256)}, u32[]{:S(2)}) copy-start(f32[256]{0:T(256)} %param.13) | copy-start | bytes 3076
  26.3 8.1 %collective-permute-start.12 = (f32[2,128,128]{2,1,0:T(8,128)S(1)}, f32[2,128,128]{2,1,0:T(8,128)S(1)}, u32[]{:S(2)}, u32[]{:S(2)}) collective-permute-start(f32[2,128,128]{2,1,0:T(8,128)S(1)} %get-tuple-element.17), channel_id=1, source_target_pairs={{0,2},{1,3},{2,4},{3,5},{4,6},{5,7},{6,0},{7,1},{8,10},{9,11},{10,... | collective-permute-start | bytes 393224 | tf_op jit(solution)/shard_map/ppermute | solution.py:131
  28.0 11.2 %collective-permute-start.13 = (f32[2,128,128]{2,1,0:T(8,128)S(1)}, f32[2,128,128]{2,1,0:T(8,128)S(1)}, u32[]{:S(2)}, u32[]{:S(2)}) collective-permute-start(f32[2,128,128]{2,1,0:T(8,128)S(1)} %get-tuple-element.19), channel_id=1, source_target_pairs={{0,4},{1,5},{2,6},{3,7},{4,0},{5,1},{6,2},{7,3},{8,12},{9,13},{10,... | collective-permute-start | bytes 393224 | tf_op jit(solution)/shard_map/ppermute | solution.py:131
  32.0 7.2 %collective-permute-start.14 = (f32[2,128,128]{2,1,0:T(8,128)S(1)}, f32[2,128,128]{2,1,0:T(8,128)S(1)}, u32[]{:S(2)}, u32[]{:S(2)}) collective-permute-start(f32[2,128,128]{2,1,0:T(8,128)S(1)} %get-tuple-element.18), channel_id=1, source_target_pairs={{0,6},{1,7},{2,0},{3,1},{4,2},{5,3},{6,4},{7,5},{8,14},{9,15},{10,... | collective-permute-start | bytes 393224 | tf_op jit(solution)/shard_map/ppermute | solution.py:131
  32.3 14.3 %collective-permute-start.10 = (f32[2,128,128]{2,1,0:T(8,128)S(1)}, f32[2,128,128]{2,1,0:T(8,128)S(1)}, u32[]{:S(2)}, u32[]{:S(2)}) collective-permute-start(f32[2,128,128]{2,1,0:T(8,128)S(1)} %get-tuple-element.21), channel_id=1, source_target_pairs={{0,6},{1,7},{2,0},{3,1},{4,2},{5,3},{6,4},{7,5},{8,14},{9,15},{10,... | collective-permute-start | bytes 393224 | tf_op jit(solution)/shard_map/ppermute | solution.py:131
  32.7 13.9 %collective-permute-start.8 = (f32[2,128,128]{2,1,0:T(8,128)S(1)}, f32[2,128,128]{2,1,0:T(8,128)S(1)}, u32[]{:S(2)}, u32[]{:S(2)}) collective-permute-start(f32[2,128,128]{2,1,0:T(8,128)S(1)} %get-tuple-element.20), channel_id=1, source_target_pairs={{0,2},{1,3},{2,4},{3,5},{4,6},{5,7},{6,0},{7,1},{8,10},{9,11},{10,... | collective-permute-start | bytes 393224 | tf_op jit(solution)/shard_map/ppermute | solution.py:131
  34.4 12.2 %collective-permute-start.9 = (f32[2,128,128]{2,1,0:T(8,128)S(1)}, f32[2,128,128]{2,1,0:T(8,128)S(1)}, u32[]{:S(2)}, u32[]{:S(2)}) collective-permute-start(f32[2,128,128]{2,1,0:T(8,128)S(1)} %get-tuple-element.22), channel_id=1, source_target_pairs={{0,4},{1,5},{2,6},{3,7},{4,0},{5,1},{6,2},{7,3},{8,12},{9,13},{10,... | collective-permute-start | bytes 393224 | tf_op jit(solution)/shard_map/ppermute | solution.py:131
  39.2 9.5 %collective-permute-start.15 = (f32[128,128]{1,0:T(8,128)S(1)}, f32[128,128]{1,0:T(8,128)S(1)}, u32[]{:S(2)}, u32[]{:S(2)}) collective-permute-start(f32[128,128]{1,0:T(8,128)S(1)} %get-tuple-element.23), channel_id=1, source_target_pairs={{0,8},{1,9},{2,10},{3,11},{4,12},{5,13},{6,14},{7,15},{8,16},{9,17... | collective-permute-start | bytes 196616 | tf_op jit(solution)/shard_map/ppermute | solution.py:140
  41.4 9.3 %collective-permute-start.16 = (f32[128,128]{1,0:T(8,128)S(1)}, f32[128,128]{1,0:T(8,128)S(1)}, u32[]{:S(2)}, u32[]{:S(2)}) collective-permute-start(f32[128,128]{1,0:T(8,128)S(1)} %get-tuple-element.24), channel_id=1, source_target_pairs={{0,16},{1,17},{2,18},{3,19},{4,20},{5,21},{6,22},{7,23},{8,24},{9,... | collective-permute-start | bytes 196616 | tf_op jit(solution)/shard_map/ppermute | solution.py:140
  46.7 6.0 %collective-permute-start.17 = (f32[128,128]{1,0:T(8,128)S(1)}, f32[128,128]{1,0:T(8,128)S(1)}, u32[]{:S(2)}, u32[]{:S(2)}) collective-permute-start(f32[128,128]{1,0:T(8,128)S(1)} %slice_bitcast_fusion), channel_id=1, source_target_pairs={{0,24},{1,25},{2,26},{3,27},{4,28},{5,29},{6,30},{7,31},{8,0},{9,1... | collective-permute-start | bytes 196616 | tf_op jit(solution)/shard_map/ppermute | solution.py:140
